TPU v7x, 512 devices: a whole 4x4x16 slice. The times are simulated.
512 devices in a mesh: pipe: 4 (over y), expert: 32 (over z, core), tensor: 4 (over x).
Axes of the slice: x: 4, y: 4, z: 16, core: 2. Of those that a mesh axis runs over, the one named last changes fastest.
Arguments:
- tokens: bfloat16 [512, 6144], P('expert', ('pipe', 'tensor')), may hold values from -6 to 6
- expert_ids: int32 [512, 2], P('expert'), may hold values from 0 to 7, all different within a row; in each aligned block of 16 rows (0 to 15, 16 to 31, ...) at most 5 rows name the same one
- gates: float32 [512, 2], P('expert'), may hold values from 0.2 to 1
- w_gate: bfloat16 [32, 6144, 2048], P('expert', None, ('pipe', 'tensor')), may hold values from -0.078125 to 0.078125
- w_up: bfloat16 [32, 6144, 2048], P('expert', None, ('pipe', 'tensor')), may hold values from -0.078125 to 0.078125
- w_down: bfloat16 [32, 2048, 6144], P('expert', ('pipe', 'tensor')), may hold values from -0.0625 to 0.0625
- d_out: bfloat16 [512, 6144], P('expert', ('pipe', 'tensor')), may hold values from -6 to 6
Outputs:
- moe_out: bfloat16 [512, 6144], P('expert', ('pipe', 'tensor'))
- grad_tokens: bfloat16 [512, 6144], P('expert', ('pipe', 'tensor'))
- grad_gates: float32 [512, 2], P('expert')
Inputs may be any that keep to these rules, and one draw needn't show every extreme that they name: `expert_ids`: each row names 2 different experts. Among the rows of one index of expert (aligned blocks of 16 rows) no expert is named more than 5 times, a bound that some block reaches.
All inputs are finite; a program needn't handle non-finite values.
Results may differ from a plain program's by a relative error of at most 0.017.
Values may be sent and summed in bfloat16 or wider, within the bound.
No kernel may reach another device: no remote copies, remote signals or barrier semaphores. Data moves between devices by JAX's collectives and lax.ppermute only.
A program may use at most 64 MiB of HBM per device.

v0:
```python
import jax
import jax.numpy as jnp
from jax import lax
from jax.sharding import PartitionSpec as P


def per_device(tokens, expert_ids, gates, w_gate, w_up, w_down, d_out):
    tok_rows = tokens.shape[0]
    top = expert_ids.shape[1]
    devices_all = lax.axis_size("expert")
    experts = min(8, devices_all)
    group = devices_all // experts
    capacity = min(
        tok_rows,
        max(2, max(5 * tok_rows * top // (4 * experts), (tok_rows * top + experts - 1) // experts)),
    )
    slots = experts * capacity
    flat_ids = expert_ids.reshape(-1)
    onehot = (flat_ids[:, None] == jnp.arange(experts, dtype=jnp.int32)[None, :]).astype(jnp.int32)
    position = jnp.sum(jnp.cumsum(onehot, axis=0) * onehot, axis=1) - 1
    slot_of = flat_ids * capacity + position
    picks = (jnp.arange(slots, dtype=jnp.int32)[:, None] == slot_of[None, :]).astype(jnp.float32)
    pick_rows = picks.reshape(slots, tok_rows, top)
    select_tok = jnp.sum(pick_rows, axis=2).astype(jnp.bfloat16)
    select_gate = jnp.sum(pick_rows * gates[None, :, :], axis=2)
    whole_x, whole_dy = (
        lax.all_gather(tokens, ("pipe", "tensor"), axis=1, tiled=True),
        lax.all_gather(d_out, ("pipe", "tensor"), axis=1, tiled=True),
    )
    picked = jnp.dot(select_tok, whole_x, preferred_element_type=jnp.float32).astype(jnp.bfloat16)
    send_x = jnp.repeat(picked.reshape(experts, capacity, -1), group, axis=0)
    scaled = jnp.dot(select_gate, whole_dy.astype(jnp.float32), precision=lax.Precision.HIGHEST)
    send_dy = jnp.repeat(scaled.astype(jnp.bfloat16).reshape(experts, capacity, -1), group, axis=0)
    recv_x, recv_dy = (
        lax.all_to_all(send_x, "expert", split_axis=0, concat_axis=0, tiled=True),
        lax.all_to_all(send_dy, "expert", split_axis=0, concat_axis=0, tiled=True),
    )
    rows_x = recv_x.reshape(devices_all * capacity, -1)
    rows_dy = recv_dy.reshape(devices_all * capacity, -1)
    gate_proj = w_gate[0]
    up_proj = w_up[0]
    down_proj = w_down[0]
    contract_last = (((1,), (1,)), ((), ()))
    h_gate = jnp.dot(rows_x, gate_proj, preferred_element_type=jnp.float32)
    h_up = jnp.dot(rows_x, up_proj, preferred_element_type=jnp.float32)
    sig = jax.nn.sigmoid(h_gate)
    hidden = (h_gate * sig * h_up).astype(jnp.bfloat16)
    out_terms = jnp.dot(hidden, down_proj, preferred_element_type=jnp.float32)
    d_hidden = lax.dot_general(
        rows_dy, down_proj, contract_last, preferred_element_type=jnp.float32
    )
    d_gate_h = (d_hidden * h_up * sig * (1.0 + h_gate * (1.0 - sig))).astype(jnp.bfloat16)
    d_up_h = (d_hidden * h_gate * sig).astype(jnp.bfloat16)
    dx_terms = lax.dot_general(
        d_gate_h, gate_proj, contract_last, preferred_element_type=jnp.float32
    )
    dx_terms = dx_terms + lax.dot_general(
        d_up_h, up_proj, contract_last, preferred_element_type=jnp.float32
    )
    out_share, dx_share = (
        lax.psum_scatter(
            out_terms.astype(jnp.bfloat16), ("pipe", "tensor"), scatter_dimension=1, tiled=True
        ).astype(jnp.float32),
        lax.psum_scatter(
            dx_terms.astype(jnp.bfloat16), ("pipe", "tensor"), scatter_dimension=1, tiled=True
        ).astype(jnp.float32),
    )
    out_slot = out_share.reshape(devices_all, capacity, -1)
    dx_slot = dx_share.reshape(devices_all, capacity, -1)
    back_out, back_dx = (
        lax.all_to_all(
            out_slot.astype(jnp.bfloat16), "expert", split_axis=0, concat_axis=0, tiled=True
        ).astype(out_slot.dtype),
        lax.all_to_all(
            dx_slot.astype(jnp.bfloat16), "expert", split_axis=0, concat_axis=0, tiled=True
        ).astype(dx_slot.dtype),
    )
    out_rows = (
        jnp.sum(back_out.reshape(experts, group, capacity, -1), axis=1)
        .astype(jnp.bfloat16)
        .reshape(slots, -1)
    )
    dx_rows = (
        jnp.sum(back_dx.reshape(experts, group, capacity, -1), axis=1)
        .astype(jnp.bfloat16)
        .reshape(slots, -1)
    )
    assign = picks.T.astype(jnp.bfloat16)
    a_out = jnp.dot(assign, out_rows, preferred_element_type=jnp.float32)
    a_dx = jnp.dot(assign, dx_rows, preferred_element_type=jnp.float32)
    a_out = a_out.reshape(tok_rows, top, -1)
    a_dx = a_dx.reshape(tok_rows, top, -1)
    moe_out = jnp.sum(gates[:, :, None] * a_out, axis=1).astype(jnp.bfloat16)
    grad_tokens = jnp.sum(a_dx, axis=1).astype(jnp.bfloat16)
    partial_dots = jnp.sum(d_out.astype(jnp.float32)[:, None, :] * a_out, axis=2)
    grad_gates = lax.psum(partial_dots, ("pipe", "tensor"))
    return (moe_out, grad_tokens, grad_gates)


def solution(mesh):
    return jax.shard_map(
        per_device,
        mesh=mesh,
        in_specs=(
            P("expert", ("pipe", "tensor")),
            P("expert", None),
            P("expert", None),
            P("expert", None, ("pipe", "tensor")),
            P("expert", None, ("pipe", "tensor")),
            P("expert", ("pipe", "tensor"), None),
            P("expert", ("pipe", "tensor")),
        ),
        out_specs=(
            P("expert", ("pipe", "tensor")),
            P("expert", ("pipe", "tensor")),
            P("expert", None),
        ),
        check_vma=False,
    )
```

profile of v0, /device:TPU:1, one launch (start us, length us, event | category | flops | bytes accessed | tf_op | source)
XLA Modules:
  0.0 608.1 jit_solution(9177753172685445268)
XLA Ops:
  7.2 0.9 copy.30
  8.6 0.7 multiply_add_fusion
  9.3 20.0 %all_gather.6 = bf16[16,6144]{1,0:T(8,128)(2,1)S(1)} all-gather(bf16[16,384]{1,0:T(8,128)(2,1)} %param.7), channel_id=1, replica_groups=mesh['pipe'=4,'expert'=32,'tensor'=4] {'pipe','tensor'}, dimensions={1}, use_global_device_ids=true | all-gather | bytes 208896 | tf_op jit(solution)/shard_map/all_gather | solution.py:27
  29.4 0.8 select_reduce_fusion
  30.7 2.0 broadcast_in_dim.4
  32.7 20.9 %all-to-all-start = ((bf16[32,5,6144]{2,1,0:T(8,128)(2,1)}), bf16[32,5,6144]{2,1,0:T(8,128)(2,1)}, u32[]{:S(2)}, u32[]{:S(2)}) async-start(bf16[32,5,6144]{2,1,0:T(8,128)(2,1)} %bitcast.42), calls=%async_computation | async-start | bytes 6291456 | tf_op jit(solution)/shard_map/all_to_all | solution.py:35
  53.6 19.3 %all_gather.7 = bf16[16,6144]{1,0:T(8,128)(2,1)S(1)} all-gather(bf16[16,384]{1,0:T(8,128)(2,1)S(1)} %copy-done.5), channel_id=1, replica_groups=mesh['pipe'=4,'expert'=32,'tensor'=4] {'pipe','tensor'}, dimensions={1}, use_global_device_ids=true | all-gather | bytes 208896 | tf_op jit(solution)/shard_map/all_gather | solution.py:28
  73.8 120.9 %all-to-all-done = bf16[32,5,6144]{2,1,0:T(8,128)(2,1)} async-done(((bf16[32,5,6144]{2,1,0:T(8,128)(2,1)}), bf16[32,5,6144]{2,1,0:T(8,128)(2,1)}, u32[]{:S(2)}, u32[]{:S(2)}) %all-to-all-start) | async-done | bytes 1966112 | tf_op jit(solution)/shard_map/all_to_all | solution.py:35
  194.6 2.1 broadcast_in_dim.5
  196.7 7.8 %all-to-all-start.2 = ((bf16[32,5,6144]{2,1,0:T(8,128)(2,1)}), bf16[32,5,6144]{2,1,0:T(8,128)(2,1)}, u32[]{:S(2)}, u32[]{:S(2)}) async-start(bf16[32,5,6144]{2,1,0:T(8,128)(2,1)} %bitcast.43), calls=%async_computation.2 | async-start | bytes 6291456 | tf_op jit(solution)/shard_map/all_to_all | solution.py:36
  204.5 3.0 reshape.130
  207.6 1.3 fusion.9
  209.0 1.3 fusion.5
  210.3 135.3 %all-to-all-done.2 = bf16[32,5,6144]{2,1,0:T(8,128)(2,1)} async-done(((bf16[32,5,6144]{2,1,0:T(8,128)(2,1)}), bf16[32,5,6144]{2,1,0:T(8,128)(2,1)}, u32[]{:S(2)}, u32[]{:S(2)}) %all-to-all-start.2) | async-done | bytes 1966112 | tf_op jit(solution)/shard_map/all_to_all | solution.py:36
  345.6 3.0 reshape.135
  348.6 2.1 fusion.1
  351.5 0.7 copy-done.2
  352.9 2.8 copy.34
  355.7 2.2 convolution_convert_fusion
  357.9 2.8 copy.32
  360.7 78.4 %reduce-scatter.9.cloned.1.call-done = bf16[384,160]{1,0:T(8,128)(2,1)} async-done(((bf16[6144,160]{1,0:T(8,128)(2,1)}), bf16[384,160]{1,0:T(8,128)(2,1)}) %reduce-scatter.9.cloned.1.call-update) | async-done | bytes 122896
  439.1 1.1 copy.35
  440.1 0.7 convert_element_type.142
  440.9 14.7 %all-to-all-start.3 = ((bf16[32,5,384]{2,1,0:T(8,128)(2,1)}), bf16[32,5,384]{2,1,0:T(8,128)(2,1)S(1)}, u32[]{:S(2)}, u32[]{:S(2)}) async-start(bf16[32,5,384]{2,1,0:T(8,128)(2,1)} %convert_element_type.142), calls=%async_computation.3 | async-start | bytes 393216 | tf_op jit(solution)/shard_map/all_to_all | solution.py:74
  455.6 78.2 %reduce-scatter.7.cloned.1.call-done = bf16[384,160]{1,0:T(8,128)(2,1)} async-done(((bf16[6144,160]{1,0:T(8,128)(2,1)}), bf16[384,160]{1,0:T(8,128)(2,1)}) %reduce-scatter.7.cloned.1.call-update) | async-done | bytes 122896
  533.8 1.1 copy.33
  534.9 0.7 convert_element_type.134
  535.6 14.7 %all-to-all-start.1 = ((bf16[32,5,384]{2,1,0:T(8,128)(2,1)}), bf16[32,5,384]{2,1,0:T(8,128)(2,1)S(1)}, u32[]{:S(2)}, u32[]{:S(2)}) async-start(bf16[32,5,384]{2,1,0:T(8,128)(2,1)} %convert_element_type.134), calls=%async_computation.1 | async-start | bytes 393216 | tf_op jit(solution)/shard_map/all_to_all | solution.py:71
  550.4 0.8 convolution_reduce_fusion
  551.2 17.7 %all-to-all-done.1 = bf16[32,5,384]{2,1,0:T(8,128)(2,1)S(1)} async-done(((bf16[32,5,384]{2,1,0:T(8,128)(2,1)}), bf16[32,5,384]{2,1,0:T(8,128)(2,1)S(1)}, u32[]{:S(2)}, u32[]{:S(2)}) %all-to-all-start.1) | async-done | bytes 122912 | tf_op jit(solution)/shard_map/all_to_all | solution.py:71
  569.0 0.9 multiply_reduce_fusion
  569.9 31.4 %psum.7 = f32[16,2]{0,1:T(2,128)} all-reduce(f32[16,2]{0,1:T(2,128)S(1)} %get-tuple-element.3), channel_id=1, replica_groups=mesh['pipe'=4,'expert'=32,'tensor'=4] {'pipe','tensor'}, use_global_device_ids=true, to_apply=%region_11.12 | all-reduce | flops 32 | bytes 256 | tf_op jit(solution)/shard_map/psum | solution.py:96
  (36 shorter events, 3.7 us)
Async XLA Ops:
  7.2 200.4 %copy-start = (bf16[1,6144,128]{2,1,0:T(8,128)(2,1)S(1)}, bf16[1,6144,128]{2,1,0:T(8,128)(2,1)}, u32[]{:S(2)}) copy-start(bf16[1,6144,128]{2,1,0:T(8,128)(2,1)} %param.10) | copy-start | bytes 4718596
  32.7 20.9 %copy-start.5 = (bf16[16,384]{1,0:T(8,128)(2,1)S(1)}, bf16[16,384]{1,0:T(8,128)(2,1)}, u32[]{:S(2)}) copy-start(bf16[16,384]{1,0:T(8,128)(2,1)} %param.13) | copy-start | bytes 36868
  32.7 161.9 %all-to-all-start = ((bf16[32,5,6144]{2,1,0:T(8,128)(2,1)}), bf16[32,5,6144]{2,1,0:T(8,128)(2,1)}, u32[]{:S(2)}, u32[]{:S(2)}) async-start(bf16[32,5,6144]{2,1,0:T(8,128)(2,1)} %bitcast.42), calls=%async_computation | async-start | bytes 6291456 | tf_op jit(solution)/shard_map/all_to_all | solution.py:35
  196.7 148.9 %all-to-all-start.2 = ((bf16[32,5,6144]{2,1,0:T(8,128)(2,1)}), bf16[32,5,6144]{2,1,0:T(8,128)(2,1)}, u32[]{:S(2)}, u32[]{:S(2)}) async-start(bf16[32,5,6144]{2,1,0:T(8,128)(2,1)} %bitcast.43), calls=%async_computation.2 | async-start | bytes 6291456 | tf_op jit(solution)/shard_map/all_to_all | solution.py:36
  204.5 234.6 %reduce-scatter.9.cloned.1.call-start = ((), (), s32[]{:S(2)}) async-start(), calls=%async_computation.7 | async-start | bytes 3342336
  207.6 1.4 copy-start.1
  348.6 2.1 copy-start.3
  348.6 2.1 copy-start.4
  350.8 1.4 copy-start.2
  355.7 178.2 %reduce-scatter.7.cloned.1.call-start = ((), (), s32[]{:S(2)}) async-start(), calls=%async_computation.6 | async-start | bytes 3342336
  360.7 208.3 %copy-start.6 = (f32[16,2]{0,1:T(2,128)S(1)}, f32[16,2]{0,1:T(2,128)}, u32[]{:S(2)}) copy-start(f32[16,2]{0,1:T(2,128)} %param.9) | copy-start | bytes 388
  440.9 94.7 %all-to-all-start.3 = ((bf16[32,5,384]{2,1,0:T(8,128)(2,1)}), bf16[32,5,384]{2,1,0:T(8,128)(2,1)S(1)}, u32[]{:S(2)}, u32[]{:S(2)}) async-start(bf16[32,5,384]{2,1,0:T(8,128)(2,1)} %convert_element_type.142), calls=%async_computation.3 | async-start | bytes 393216 | tf_op jit(solution)/shard_map/all_to_all | solution.py:74
  535.6 33.3 %all-to-all-start.1 = ((bf16[32,5,384]{2,1,0:T(8,128)(2,1)}), bf16[32,5,384]{2,1,0:T(8,128)(2,1)S(1)}, u32[]{:S(2)}, u32[]{:S(2)}) async-start(bf16[32,5,384]{2,1,0:T(8,128)(2,1)} %convert_element_type.134), calls=%async_computation.1 | async-start | bytes 393216 | tf_op jit(solution)/shard_map/all_to_all | solution.py:71
Sparse Core Ops, SparseCore 0:
  355.8 83.2 reduce-scatter.8
  443.3 90.4 reduce-scatter.6
where the time goes:
time: 615 us; the launch traced here: 608 us
  waiting for transfers between devices  431 us (70%)
  blocking collectives  70.7 us (11%)
  starting transfers between devices  58.2 us (9%)
  local copies, waits for them, and re-layouts  21.7 us (4%)
  between operations  14.3 us (2%)
  matrix products  10.8 us (2%)
    unnamed x4, waiting for transfers between devices  157 us
    all_to_all x1, waiting for transfers between devices, per_device(): lax.all_to_all(send_dy, 'expert', split_axis=0, concat_axis=0, tiled=True)  135 us
    all_to_all x1, waiting for transfers between devices, per_device(): lax.all_to_all(send_x, 'expert', split_axis=0, concat_axis=0, tiled=True)  121 us
    psum x1, blocking collectives, per_device(): grad_gates = lax.psum(partial_dots, ('pipe', 'tensor'))  31.4 us
    all_to_all x1, starting transfers between devices, per_device(): lax.all_to_all(send_x, 'expert', split_axis=0, concat_axis=0, tiled=True)  20.9 us
    all_gather x1, blocking collectives, per_device(): lax.all_gather(tokens, ('pipe', 'tensor'), axis=1, tiled=True)  20 us
    all_gather x1, blocking collectives, per_device(): lax.all_gather(d_out, ('pipe', 'tensor'), axis=1, tiled=True)  19.3 us
    all_to_all x1, waiting for transfers between devices, per_device(): lax.all_to_all(out_slot.astype(jnp.bfloat16), 'expert', split_axis=0, con...  17.7 us
  transfers between devices with their start and end apart: 6, of which 5 were waited for; matrix products, arithmetic and copies ran while one was open for 3% of the time, Pallas kernels for 0%

commit v1 on v0

v1 whole, which is shorter than its diff:
```python
import jax
import jax.numpy as jnp
from jax import lax
from jax.sharding import PartitionSpec as P


def per_device(tokens, expert_ids, gates, w_gate, w_up, w_down, d_out):
    tok_rows = tokens.shape[0]
    feat = tokens.shape[1]
    top = expert_ids.shape[1]
    devices_all = lax.axis_size("expert")
    experts = min(8, devices_all)
    group = devices_all // experts
    capacity = min(
        tok_rows,
        max(2, max(5 * tok_rows * top // (4 * experts), (tok_rows * top + experts - 1) // experts)),
    )
    slots = experts * capacity
    flat_ids = expert_ids.reshape(-1)
    onehot = (flat_ids[:, None] == jnp.arange(experts, dtype=jnp.int32)[None, :]).astype(jnp.int32)
    position = jnp.sum(jnp.cumsum(onehot, axis=0) * onehot, axis=1) - 1
    slot_of = flat_ids * capacity + position
    picks = (jnp.arange(slots, dtype=jnp.int32)[:, None] == slot_of[None, :]).astype(jnp.float32)
    pick_rows = picks.reshape(slots, tok_rows, top)
    select_tok = jnp.sum(pick_rows, axis=2).astype(jnp.bfloat16)
    select_gate = jnp.sum(pick_rows * gates[None, :, :], axis=2)
    picked = jnp.dot(select_tok, tokens, preferred_element_type=jnp.float32).astype(jnp.bfloat16)
    scaled = jnp.dot(
        select_gate, d_out.astype(jnp.float32), precision=lax.Precision.HIGHEST
    ).astype(jnp.bfloat16)
    send = jnp.concatenate([picked, scaled], axis=1).reshape(experts, capacity, 2 * feat)
    send = jnp.repeat(send, group, axis=0)
    recv = lax.all_to_all(send, "expert", split_axis=0, concat_axis=0, tiled=True)
    recv = recv.reshape(devices_all * capacity, 2 * feat)
    part_x = recv[:, :feat]
    part_dy = recv[:, feat:]
    rows_x = lax.all_gather(part_x, ("pipe", "tensor"), axis=1, tiled=True)
    rows_dy = lax.all_gather(part_dy, ("pipe", "tensor"), axis=1, tiled=True)
    gate_proj = w_gate[0]
    up_proj = w_up[0]
    down_proj = w_down[0]
    contract_last = (((1,), (1,)), ((), ()))
    h_gate = jnp.dot(rows_x, gate_proj, preferred_element_type=jnp.float32)
    h_up = jnp.dot(rows_x, up_proj, preferred_element_type=jnp.float32)
    sig = jax.nn.sigmoid(h_gate)
    hidden = (h_gate * sig * h_up).astype(jnp.bfloat16)
    out_terms = jnp.dot(hidden, down_proj, preferred_element_type=jnp.float32)
    d_hidden = lax.dot_general(
        rows_dy, down_proj, contract_last, preferred_element_type=jnp.float32
    )
    d_gate_h = (d_hidden * h_up * sig * (1.0 + h_gate * (1.0 - sig))).astype(jnp.bfloat16)
    d_up_h = (d_hidden * h_gate * sig).astype(jnp.bfloat16)
    dx_terms = lax.dot_general(
        d_gate_h, gate_proj, contract_last, preferred_element_type=jnp.float32
    )
    dx_terms = dx_terms + lax.dot_general(
        d_up_h, up_proj, contract_last, preferred_element_type=jnp.float32
    )
    out_share = lax.psum_scatter(
        out_terms.astype(jnp.bfloat16), ("pipe", "tensor"), scatter_dimension=1, tiled=True
    )
    dx_share = lax.psum_scatter(
        dx_terms.astype(jnp.bfloat16), ("pipe", "tensor"), scatter_dimension=1, tiled=True
    )
    back_send = jnp.concatenate([out_share, dx_share], axis=1).reshape(
        devices_all, capacity, 2 * feat
    )
    back = lax.all_to_all(back_send, "expert", split_axis=0, concat_axis=0, tiled=True)
    back_rows = (
        jnp.sum(back.astype(jnp.float32).reshape(experts, group, capacity, 2 * feat), axis=1)
        .astype(jnp.bfloat16)
        .reshape(slots, 2 * feat)
    )
    assign = picks.T.astype(jnp.bfloat16)
    a_both = jnp.dot(assign, back_rows, preferred_element_type=jnp.float32)
    a_out = a_both[:, :feat].reshape(tok_rows, top, feat)
    a_dx = a_both[:, feat:].reshape(tok_rows, top, feat)
    moe_out = jnp.sum(gates[:, :, None] * a_out, axis=1).astype(jnp.bfloat16)
    grad_tokens = jnp.sum(a_dx, axis=1).astype(jnp.bfloat16)
    partial_dots = jnp.sum(d_out.astype(jnp.float32)[:, None, :] * a_out, axis=2)
    grad_gates = lax.psum(partial_dots, ("pipe", "tensor"))
    return (moe_out, grad_tokens, grad_gates)


def solution(mesh):
    return jax.shard_map(
        per_device,
        mesh=mesh,
        in_specs=(
            P("expert", ("pipe", "tensor")),
            P("expert", None),
            P("expert", None),
            P("expert", None, ("pipe", "tensor")),
            P("expert", None, ("pipe", "tensor")),
            P("expert", ("pipe", "tensor"), None),
            P("expert", ("pipe", "tensor")),
        ),
        out_specs=(
            P("expert", ("pipe", "tensor")),
            P("expert", ("pipe", "tensor")),
            P("expert", None),
        ),
        check_vma=False,
    )
```

time: 615 us -> 458 us (0.74)
  waiting for transfers between devices: 431 us -> 319 us
  starting transfers between devices: 58.2 us -> 14.9 us
  local copies, waits for them, and re-layouts: 21.7 us -> 12.2 us
    all_to_all x4 -> x1, waiting for transfers between devices: 274 us -> 27.8 us  [per_device(): lax.all_to_all(back_send, 'expert', split_axis=0, concat_axis=0, tiled=True)]
    all_gather x0 -> x2, waiting for transfers between devices: none -> 112 us  [the longest x1 60.3 us: per_device(): rows_dy = lax.all_gather(part_dy, ('pipe', 'tensor'), axis=1, tiled=True)]
    all_to_all x0 -> x1, blocking collectives: none -> 44.5 us  [per_device(): lax.all_to_all(send, 'expert', split_axis=0, concat_axis=0, tiled=True)]
    all_to_all x4 -> x1, starting transfers between devices: 58.1 us -> 14.7 us  [per_device(): lax.all_to_all(back_send, 'expert', split_axis=0, concat_axis=0, tiled=True)]
    all_gather x2 -> x0, blocking collectives: 39.3 us -> none  [the longest x1 20 us: per_device(): lax.all_gather(tokens, ('pipe', 'tensor'), axis=1, tiled=True)]
    unnamed x4 -> x6, waiting for transfers between devices: 157 us -> 179 us
  transfers between devices with their start and end apart: 6 -> 5, of which waited for: 5 -> 5; matrix products, arithmetic and copies ran while one was open for 3% -> 2% of each run, Pallas kernels for 0% -> 0%
where the time goes in v1:
time: 458 us; the launch traced here: 453 us
  waiting for transfers between devices  319 us (70%)
  blocking collectives  75.9 us (17%)
  starting transfers between devices  14.9 us (3%)
  between operations  14 us (3%)
  matrix products  13.2 us (3%)
  local copies, waits for them, and re-layouts  12.2 us (3%)
    unnamed x6, waiting for transfers between devices  179 us
    all_gather x1, waiting for transfers between devices, per_device(): rows_dy = lax.all_gather(part_dy, ('pipe', 'tensor'), axis=1, tiled=True)  60.3 us
    all_gather x1, waiting for transfers between devices, per_device(): rows_x = lax.all_gather(part_x, ('pipe', 'tensor'), axis=1, tiled=True)  52.1 us
    all_to_all x1, blocking collectives, per_device(): lax.all_to_all(send, 'expert', split_axis=0, concat_axis=0, tiled=True)  44.5 us
    psum x1, blocking collectives, per_device(): grad_gates = lax.psum(partial_dots, ('pipe', 'tensor'))  31.4 us
    all_to_all x1, waiting for transfers between devices, per_device(): lax.all_to_all(back_send, 'expert', split_axis=0, concat_axis=0, tiled=True)  27.8 us
    all_to_all x1, starting transfers between devices, per_device(): lax.all_to_all(back_send, 'expert', split_axis=0, concat_axis=0, tiled=True)  14.7 us
    unnamed x23, local copies, waits for them, and re-layouts  9.97 us
  transfers between devices with their start and end apart: 5, of which 5 were waited for; matrix products, arithmetic and copies ran while one was open for 2% of the time, Pallas kernels for 0%

profile of v1, /device:TPU:1, one launch (start us, length us, event | category | flops | bytes accessed | tf_op | source)
XLA Modules:
  0.0 452.8 jit_solution(14242704866884179317)
XLA Ops:
  7.2 0.9 copy.35
  8.3 0.2 select_reduce_fusion.1
  8.7 0.7 multiply_add_fusion
  9.4 0.8 convert_reduce_fusion
  10.1 0.9 convolution_convert_fusion.1
  11.1 0.9 convolution_convert_fusion.2
  12.1 44.5 %all_to_all.10 = bf16[32,5,768]{2,1,0:T(8,128)(2,1)S(1)} all-to-all(bf16[32,5,768]{2,1,0:T(8,128)(2,1)S(1)} %bitcast.32), channel_id=1, replica_groups=mesh['pipe'=4,'expert'=32,'tensor'=4] {'expert'}, dimensions={0} | all-to-all | bytes 491520 | tf_op jit(solution)/shard_map/all_to_all | solution.py:33
  56.7 0.7 fusion.21
  57.5 0.7 all-gather.5.cloned.1.call-update
  58.3 52.1 %all-gather.3.cloned.1.call-done = bf16[160,6144]{1,0:T(8,128)(2,1)} async-done(((bf16[160,384]{1,0:T(8,128)(2,1)}), bf16[160,6144]{1,0:T(8,128)(2,1)}) %all-gather.3.cloned.1.call-update) | async-done | bytes 1966096 | tf_op jit(solution)/shard_map/all_gather | solution.py:37
  110.4 2.3 fusion.9
  112.7 2.2 fusion.5
  115.0 60.3 %all-gather.5.cloned.1.call-done = bf16[160,6144]{1,0:T(8,128)(2,1)} async-done(((bf16[160,384]{1,0:T(8,128)(2,1)}), bf16[160,6144]{1,0:T(8,128)(2,1)}) %all-gather.5.cloned.1.call-update) | async-done | bytes 1966096 | tf_op jit(solution)/shard_map/all_gather | solution.py:38
  175.2 2.2 fusion.1
  177.5 0.7 fusion.7
  178.2 0.7 copy-done.3
  178.9 1.6 fusion
  180.4 2.8 copy.40
  183.3 2.2 convolution_convert_fusion
  185.4 2.8 copy.38
  188.3 84.8 %reduce-scatter.9.cloned.1.call-done = bf16[384,160]{1,0:T(8,128)(2,1)} async-done(((bf16[6144,160]{1,0:T(8,128)(2,1)}), bf16[384,160]{1,0:T(8,128)(2,1)}) %reduce-scatter.9.cloned.1.call-update) | async-done | bytes 122896
  273.1 1.1 copy.41
  274.2 93.5 %reduce-scatter.7.cloned.1.call-done = bf16[384,160]{1,0:T(8,128)(2,1)} async-done(((bf16[6144,160]{1,0:T(8,128)(2,1)}), bf16[384,160]{1,0:T(8,128)(2,1)}) %reduce-scatter.7.cloned.1.call-update) | async-done | bytes 122896
  367.7 1.1 copy.39
  368.7 0.8 reshape.67
  369.6 14.7 %all-to-all-start.1 = ((bf16[32,5,768]{2,1,0:T(8,128)(2,1)}), bf16[32,5,768]{2,1,0:T(8,128)(2,1)S(1)}, u32[]{:S(2)}, u32[]{:S(2)}) async-start(bf16[32,5,768]{2,1,0:T(8,128)(2,1)} %reshape.67), calls=%async_computation.1 | async-start | bytes 786432 | tf_op jit(solution)/shard_map/all_to_all | solution.py:68
  384.4 27.8 %all-to-all-done.1 = bf16[32,5,768]{2,1,0:T(8,128)(2,1)S(1)} async-done(((bf16[32,5,768]{2,1,0:T(8,128)(2,1)}), bf16[32,5,768]{2,1,0:T(8,128)(2,1)S(1)}, u32[]{:S(2)}, u32[]{:S(2)}) %all-to-all-start.1) | async-done | bytes 245792 | tf_op jit(solution)/shard_map/all_to_all | solution.py:68
  412.4 0.2 fusion.15
  412.9 31.4 %psum.7 = f32[16,2]{1,0:T(8,128)S(1)} all-reduce(f32[16,2]{1,0:T(8,128)S(1)} %reduce_sum.72), channel_id=1, replica_groups=mesh['pipe'=4,'expert'=32,'tensor'=4] {'pipe','tensor'}, use_global_device_ids=true, to_apply=%region_10.11 | all-reduce | flops 32 | bytes 256 | tf_op jit(solution)/shard_map/psum | solution.py:81
  444.3 0.6 copy.37
  444.9 0.7 multiply_reduce_fusion.1
  445.6 0.7 reduce_sum.70
  (42 shorter events, 1.4 us)
Async XLA Ops:
  7.2 103.2 %copy-start = (bf16[1,6144,128]{2,1,0:T(8,128)(2,1)S(1)}, bf16[1,6144,128]{2,1,0:T(8,128)(2,1)}, u32[]{:S(2)}) copy-start(bf16[1,6144,128]{2,1,0:T(8,128)(2,1)} %param.10) | copy-start | bytes 4718596
  7.2 103.2 %all-gather.3.cloned.1.call-start = ((), (), s32[]{:S(2)}) async-start(), calls=%async_computation.4 | async-start | bytes 2088960 | tf_op jit(solution)/shard_map/all_gather | solution.py:37
  57.5 117.8 %all-gather.5.cloned.1.call-start = ((), (), s32[]{:S(2)}) async-start(), calls=%async_computation.5 | async-start | bytes 2088960 | tf_op jit(solution)/shard_map/all_gather | solution.py:38
  58.2 214.9 %reduce-scatter.9.cloned.1.call-start = ((), (), s32[]{:S(2)}) async-start(), calls=%async_computation.7 | async-start | bytes 3342336
  110.4 2.4 copy-start.1
  112.7 64.7 %copy-start.4 = (f32[160,128]{1,0:T(8,128)}, f32[160,128]{1,0:T(8,128)S(1)}, u32[]{:S(2)}) copy-start(f32[160,128]{1,0:T(8,128)S(1)} %fusion.9) | copy-start | bytes 245764
  112.7 62.5 %copy-start.2 = (bf16[1,128,6144]{2,1,0:T(8,128)(2,1)S(1)}, bf16[1,128,6144]{2,1,0:T(8,128)(2,1)}, u32[]{:S(2)}) copy-start(bf16[1,128,6144]{2,1,0:T(8,128)(2,1)} %param.12) | copy-start | bytes 4718596
  114.9 62.5 %copy-start.5 = (f32[160,128]{1,0:T(8,128)}, f32[160,128]{1,0:T(8,128)S(1)}, u32[]{:S(2)}) copy-start(f32[160,128]{1,0:T(8,128)S(1)} %fusion.5) | copy-start | bytes 245764
  177.5 1.4 copy-start.3
  183.2 184.4 %reduce-scatter.7.cloned.1.call-start = ((), (), s32[]{:S(2)}) async-start(), calls=%async_computation.6 | async-start | bytes 3342336
  188.2 196.0 %copy-start.7 = (f32[16,2]{0,1:T(2,128)S(1)}, f32[16,2]{0,1:T(2,128)}, u32[]{:S(2)}) copy-start(f32[16,2]{0,1:T(2,128)} %param.9) | copy-start | bytes 388
  188.3 196.1 %copy-start.6 = (bf16[16,384]{1,0:T(8,128)(2,1)S(1)}, bf16[16,384]{1,0:T(8,128)(2,1)}, u32[]{:S(2)}) copy-start(bf16[16,384]{1,0:T(8,128)(2,1)} %param.13) | copy-start | bytes 36868
  369.6 42.7 %all-to-all-start.1 = ((bf16[32,5,768]{2,1,0:T(8,128)(2,1)}), bf16[32,5,768]{2,1,0:T(8,128)(2,1)S(1)}, u32[]{:S(2)}, u32[]{:S(2)}) async-start(bf16[32,5,768]{2,1,0:T(8,128)(2,1)} %reshape.67), calls=%async_computation.1 | async-start | bytes 786432 | tf_op jit(solution)/shard_map/all_to_all | solution.py:68
Sparse Core Ops, SparseCore 0:
  57.6 52.7 all-gather.2
  113.3 61.8 all-gather.4
  183.3 89.7 reduce-scatter.8
  277.2 90.4 reduce-scatter.6

commit v2 on v1

--- a/solution.py
+++ b/solution.py
@@ -32,10 +32,11 @@
     send = jnp.repeat(send, group, axis=0)
     recv = lax.all_to_all(send, "expert", split_axis=0, concat_axis=0, tiled=True)
     recv = recv.reshape(devices_all * capacity, 2 * feat)
-    part_x = recv[:, :feat]
-    part_dy = recv[:, feat:]
-    rows_x = lax.all_gather(part_x, ("pipe", "tensor"), axis=1, tiled=True)
-    rows_dy = lax.all_gather(part_dy, ("pipe", "tensor"), axis=1, tiled=True)
+    planes = lax.axis_size("pipe") * lax.axis_size("tensor")
+    spread = jnp.broadcast_to(recv[None], (planes,) + recv.shape)
+    gathered = lax.all_to_all(spread, ("pipe", "tensor"), 0, 0, tiled=True)
+    rows_x = gathered[:, :, :feat].transpose(1, 0, 2).reshape(devices_all * capacity, planes * feat)
+    rows_dy = gathered[:, :, feat:].transpose(1, 0, 2).reshape(devices_all * capacity, planes * feat)
     gate_proj = w_gate[0]
     up_proj = w_up[0]
     down_proj = w_down[0]
@@ -56,15 +57,17 @@
     dx_terms = dx_terms + lax.dot_general(
         d_up_h, up_proj, contract_last, preferred_element_type=jnp.float32
     )
-    out_share = lax.psum_scatter(
-        out_terms.astype(jnp.bfloat16), ("pipe", "tensor"), scatter_dimension=1, tiled=True
-    )
-    dx_share = lax.psum_scatter(
-        dx_terms.astype(jnp.bfloat16), ("pipe", "tensor"), scatter_dimension=1, tiled=True
-    )
-    back_send = jnp.concatenate([out_share, dx_share], axis=1).reshape(
-        devices_all, capacity, 2 * feat
-    )
+    rows_n = devices_all * capacity
+    terms = jnp.concatenate(
+        [
+            out_terms.astype(jnp.bfloat16).reshape(rows_n, planes, feat),
+            dx_terms.astype(jnp.bfloat16).reshape(rows_n, planes, feat),
+        ],
+        axis=2,
+    ).transpose(1, 0, 2)
+    reduced = lax.all_to_all(terms, ("pipe", "tensor"), 0, 0, tiled=True)
+    shares = jnp.sum(reduced.astype(jnp.float32), axis=0).astype(jnp.bfloat16)
+    back_send = shares.reshape(devices_all, capacity, 2 * feat)
     back = lax.all_to_all(back_send, "expert", split_axis=0, concat_axis=0, tiled=True)
     back_rows = (
         jnp.sum(back.astype(jnp.float32).reshape(experts, group, capacity, 2 * feat), axis=1)

time: 458 us -> 239 us (0.52)
  the two profiles are of different devices: /device:TPU:1 before, /device:TPU:2 now
where the time goes in v2:
time: 239 us; the launch traced here: 238 us
  blocking collectives  186 us (78%)
  waiting for transfers between devices  28.1 us (12%)
  other arithmetic  6.53 us (3%)
  matrix products  6.15 us (3%)
  local copies, waits for them, and re-layouts  6.02 us (3%)
  starting transfers between devices  4.52 us (2%)
    all_to_all x1, blocking collectives, per_device(): gathered = lax.all_to_all(spread, ('pipe', 'tensor'), 0, 0, tiled=True)  54.1 us
    all_to_all x1, blocking collectives, per_device(): reduced = lax.all_to_all(terms, ('pipe', 'tensor'), 0, 0, tiled=True)  51.1 us
    all_to_all x1, blocking collectives, per_device(): lax.all_to_all(send, 'expert', split_axis=0, concat_axis=0, tiled=True)  43.5 us
    psum x1, blocking collectives, per_device(): grad_gates = lax.psum(partial_dots, ('pipe', 'tensor'))  37.4 us
    all_to_all x1, waiting for transfers between devices, per_device(): lax.all_to_all(back_send, 'expert', split_axis=0, concat_axis=0, tiled=True)  28.1 us
  transfers between devices with their start and end apart: 1, of which 1 were waited for; matrix products, arithmetic and copies ran while one was open for 0% of the time, Pallas kernels for 0%

profile of v2, /device:TPU:2, one launch (start us, length us, event | category | flops | bytes accessed | tf_op | source)
XLA Modules:
  0.0 238.3 jit_solution(14824726134176719293)
XLA Ops:
  0.6 0.9 copy.43
  1.7 0.2 select_reduce_fusion.1
  2.1 0.7 multiply_add_fusion
  2.8 0.8 convert_reduce_fusion
  3.6 0.9 convolution_convert_fusion.1
  4.5 0.9 convolution_convert_fusion.2
  5.5 43.5 %all_to_all.20 = bf16[32,5,768]{2,1,0:T(8,128)(2,1)S(1)} all-to-all(bf16[32,5,768]{2,1,0:T(8,128)(2,1)S(1)} %bitcast.47), channel_id=1, replica_groups=mesh['pipe'=4,'expert'=32,'tensor'=4] {'expert'}, dimensions={0} | all-to-all | bytes 491520 | tf_op jit(solution)/shard_map/all_to_all | solution.py:33
  49.1 0.4 broadcast_in_dim.8
  49.5 54.1 %all_to_all.21 = bf16[16,160,768]{2,1,0:T(8,128)(2,1)S(1)} all-to-all(bf16[16,160,768]{2,1,0:T(8,128)(2,1)S(1)} %broadcast_in_dim.8), channel_id=1, replica_groups=mesh['pipe'=4,'expert'=32,'tensor'=4] {'pipe','tensor'}, dimensions={0} | all-to-all | bytes 7864320 | tf_op jit(solution)/shard_map/all_to_all | solution.py:37
  103.6 0.4 slice_bitcast_fusion
  104.1 0.3 copy.52
  104.4 1.1 copy-done.1
  105.5 0.7 fusion.9
  106.2 0.7 fusion.5
  106.9 0.3 copy.53
  107.2 0.7 fusion.1
  107.9 0.7 convolution_convert_fusion
  108.6 0.7 fusion.7
  109.3 0.7 fusion
  110.0 0.4 copy_bitcast_fusion
  110.4 0.4 maximum_bitcast_fusion
  110.9 51.1 %all_to_all.22 = bf16[16,160,768]{2,1,0:T(8,128)(2,1)} all-to-all(bf16[16,160,768]{2,1,0:T(8,128)(2,1)S(1)} %maximum_bitcast_fusion), channel_id=1, replica_groups=mesh['pipe'=4,'expert'=32,'tensor'=4] {'pipe','tensor'}, dimensions={0} | all-to-all | bytes 7864320 | tf_op jit(solution)/shard_map/all_to_all | solution.py:68
  161.9 2.7 %reduce_sum.80 = bf16[160,768]{1,0:T(8,128)(2,1)S(1)} reduce(bf16[16,160,768]{2,1,0:T(8,128)(2,1)} %all_to_all.22, bf16[]{:T(256)} %constant.17.clone.1), dimensions={0}, to_apply=%region_4.5 | reduce | flops 1843200 | bytes 4177922 | tf_op jit(solution)/shard_map/reduce_sum | solution.py:69
  164.7 0.8 reshape.80
  165.5 4.5 %all-to-all-start.3 = ((bf16[32,5,768]{2,1,0:T(8,128)(2,1)}), bf16[32,5,768]{2,1,0:T(8,128)(2,1)S(1)}, u32[]{:S(2)}, u32[]{:S(2)}) async-start(bf16[32,5,768]{2,1,0:T(8,128)(2,1)} %reshape.80), calls=%async_computation.3 | async-start | bytes 786432 | tf_op jit(solution)/shard_map/all_to_all | solution.py:71
  170.2 28.1 %all-to-all-done.3 = bf16[32,5,768]{2,1,0:T(8,128)(2,1)S(1)} async-done(((bf16[32,5,768]{2,1,0:T(8,128)(2,1)}), bf16[32,5,768]{2,1,0:T(8,128)(2,1)S(1)}, u32[]{:S(2)}, u32[]{:S(2)}) %all-to-all-start.3) | async-done | bytes 245792 | tf_op jit(solution)/shard_map/all_to_all | solution.py:71
  198.4 0.2 fusion.15
  198.6 0.1 multiply_reduce_fusion
  198.9 37.4 %psum.7 = f32[16,2]{1,0:T(8,128)S(1)} all-reduce(f32[16,2]{1,0:T(8,128)S(1)} %reduce_sum.85), channel_id=1, replica_groups=mesh['pipe'=4,'expert'=32,'tensor'=4] {'pipe','tensor'}, use_global_device_ids=true, to_apply=%region_9.10 | all-reduce | flops 32 | bytes 256 | tf_op jit(solution)/shard_map/psum | solution.py:84
  236.3 0.6 copy.49
  236.9 0.7 multiply_reduce_fusion.1
  237.6 0.7 reduce_sum.83
  (27 shorter events, 1.0 us)
Async XLA Ops:
  0.6 106.6 %copy-start = (bf16[1,128,6144]{2,1,0:T(8,128)(2,1)S(1)}, bf16[1,128,6144]{2,1,0:T(8,128)(2,1)}, u32[]{:S(2)}) copy-start(bf16[1,128,6144]{2,1,0:T(8,128)(2,1)} %param.12) | copy-start | bytes 4718596
  104.1 1.4 copy-start.1
  104.4 1.8 copy-start.2
  161.9 8.1 %copy-start.4 = (f32[16,2]{0,1:T(2,128)S(1)}, f32[16,2]{0,1:T(2,128)}, u32[]{:S(2)}) copy-start(f32[16,2]{0,1:T(2,128)} %param.9) | copy-start | bytes 388
  161.9 8.2 %copy-start.3 = (bf16[16,384]{1,0:T(8,128)(2,1)S(1)}, bf16[16,384]{1,0:T(8,128)(2,1)}, u32[]{:S(2)}) copy-start(bf16[16,384]{1,0:T(8,128)(2,1)} %param.13) | copy-start | bytes 36868
  165.5 32.8 %all-to-all-start.3 = ((bf16[32,5,768]{2,1,0:T(8,128)(2,1)}), bf16[32,5,768]{2,1,0:T(8,128)(2,1)S(1)}, u32[]{:S(2)}, u32[]{:S(2)}) async-start(bf16[32,5,768]{2,1,0:T(8,128)(2,1)} %reshape.80), calls=%async_computation.3 | async-start | bytes 786432 | tf_op jit(solution)/shard_map/all_to_all | solution.py:71

commit v3 on v2

--- a/solution.py
+++ b/solution.py
@@ -81,7 +81,8 @@
     moe_out = jnp.sum(gates[:, :, None] * a_out, axis=1).astype(jnp.bfloat16)
     grad_tokens = jnp.sum(a_dx, axis=1).astype(jnp.bfloat16)
     partial_dots = jnp.sum(d_out.astype(jnp.float32)[:, None, :] * a_out, axis=2)
-    grad_gates = lax.psum(partial_dots, ("pipe", "tensor"))
+    dots_spread = jnp.broadcast_to(partial_dots[None], (planes,) + partial_dots.shape)
+    grad_gates = jnp.sum(lax.all_to_all(dots_spread, ("pipe", "tensor"), 0, 0, tiled=True), axis=0)
     return (moe_out, grad_tokens, grad_gates)
 
 

time: 239 us -> 212 us (0.89)
  the two profiles are of different devices: /device:TPU:2 before, /device:TPU:1 now
where the time goes in v3:
time: 212 us
  blocking collectives  148 us (70%)
  waiting for transfers between devices  32.8 us (15%)
  starting transfers between devices  10.5 us (5%)
  other arithmetic  7.12 us (3%)
  matrix products  6.16 us (3%)
  local copies, waits for them, and re-layouts  6.08 us (3%)
    all_to_all x1, blocking collectives, per_device(): gathered = lax.all_to_all(spread, ('pipe', 'tensor'), 0, 0, tiled=True)  53.9 us
    all_to_all x1, blocking collectives, per_device(): reduced = lax.all_to_all(terms, ('pipe', 'tensor'), 0, 0, tiled=True)  49.9 us
    all_to_all x1, blocking collectives, per_device(): lax.all_to_all(send, 'expert', split_axis=0, concat_axis=0, tiled=True)  44.5 us
    all_to_all x1, waiting for transfers between devices, per_device(): lax.all_to_all(back_send, 'expert', split_axis=0, concat_axis=0, tiled=True)  27.8 us
    all_to_all x1, starting transfers between devices, per_device(): lax.all_to_all(back_send, 'expert', split_axis=0, concat_axis=0, tiled=True)  7.01 us
    all_to_all x1, waiting for transfers between devices, per_device(): lax.all_to_all(dots_spread, ('pipe', 'tensor'), 0, 0, tiled=True)  4.94 us
  transfers between devices with their start and end apart: 2, of which 2 were waited for; matrix products, arithmetic and copies ran while one was open for 1% of the time, Pallas kernels for 0%

profile of v3, /device:TPU:1, one launch (start us, length us, event | category | flops | bytes accessed | tf_op | source)
XLA Modules:
  0.0 211.9 jit_solution(5536139585434314530)
XLA Ops:
  0.6 0.9 copy.41
  2.1 0.7 multiply_add_fusion
  2.8 0.8 convert_reduce_fusion
  3.6 0.9 convolution_convert_fusion.1
  4.5 0.9 convolution_convert_fusion.2
  5.5 44.5 %all_to_all.25 = bf16[32,5,768]{2,1,0:T(8,128)(2,1)S(1)} all-to-all(bf16[32,5,768]{2,1,0:T(8,128)(2,1)S(1)} %bitcast.47), channel_id=1, replica_groups=mesh['pipe'=4,'expert'=32,'tensor'=4] {'expert'}, dimensions={0} | all-to-all | bytes 491520 | tf_op jit(solution)/shard_map/all_to_all | solution.py:33
  50.1 0.4 broadcast_in_dim.12
  50.5 53.9 %all_to_all.26 = bf16[16,160,768]{2,1,0:T(8,128)(2,1)S(1)} all-to-all(bf16[16,160,768]{2,1,0:T(8,128)(2,1)S(1)} %broadcast_in_dim.12), channel_id=1, replica_groups=mesh['pipe'=4,'expert'=32,'tensor'=4] {'pipe','tensor'}, dimensions={0} | all-to-all | bytes 7864320 | tf_op jit(solution)/shard_map/all_to_all | solution.py:37
  104.5 0.4 slice_bitcast_fusion
  104.9 0.3 copy.50
  105.2 1.1 copy-done.1
  106.3 0.7 fusion.9
  107.0 0.7 fusion.5
  107.7 0.3 copy.51
  108.0 0.7 fusion.1
  108.7 0.7 convolution_convert_fusion
  109.4 0.7 fusion.7
  110.1 0.7 fusion
  110.8 0.4 copy_bitcast_fusion
  111.3 0.4 maximum_bitcast_fusion
  111.7 49.9 %all_to_all.27 = bf16[16,160,768]{2,1,0:T(8,128)(2,1)} all-to-all(bf16[16,160,768]{2,1,0:T(8,128)(2,1)S(1)} %maximum_bitcast_fusion), channel_id=1, replica_groups=mesh['pipe'=4,'expert'=32,'tensor'=4] {'pipe','tensor'}, dimensions={0} | all-to-all | bytes 7864320 | tf_op jit(solution)/shard_map/all_to_all | solution.py:68
  161.6 2.7 %reduce_sum.87 = bf16[160,768]{1,0:T(8,128)(2,1)S(1)} reduce(bf16[16,160,768]{2,1,0:T(8,128)(2,1)} %all_to_all.27, bf16[]{:T(256)} %constant.17.clone.1), dimensions={0}, to_apply=%region_4.5 | reduce | flops 1843200 | bytes 4177922 | tf_op jit(solution)/shard_map/reduce_sum | solution.py:69
  164.4 0.8 reshape.82
  165.2 7.0 %all-to-all-start.3 = ((bf16[32,5,768]{2,1,0:T(8,128)(2,1)}), bf16[32,5,768]{2,1,0:T(8,128)(2,1)S(1)}, u32[]{:S(2)}, u32[]{:S(2)}) async-start(bf16[32,5,768]{2,1,0:T(8,128)(2,1)} %reshape.82), calls=%async_computation.3 | async-start | bytes 786432 | tf_op jit(solution)/shard_map/all_to_all | solution.py:71
  172.4 27.8 %all-to-all-done.3 = bf16[32,5,768]{2,1,0:T(8,128)(2,1)S(1)} async-done(((bf16[32,5,768]{2,1,0:T(8,128)(2,1)}), bf16[32,5,768]{2,1,0:T(8,128)(2,1)S(1)}, u32[]{:S(2)}, u32[]{:S(2)}) %all-to-all-start.3) | async-done | bytes 245792 | tf_op jit(solution)/shard_map/all_to_all | solution.py:71
  200.3 0.2 fusion.15
  200.8 0.6 broadcast_in_dim.28
  201.5 3.5 %all-to-all-start.4 = ((f32[16,16,2]{1,2,0:T(2,128)}), f32[16,16,2]{1,2,0:T(2,128)S(1)}, u32[]{:S(2)}, u32[]{:S(2)}) async-start(f32[16,16,2]{1,2,0:T(2,128)} %broadcast_in_dim.28), calls=%async_computation.4 | async-start | bytes 32768 | tf_op jit(solution)/shard_map/all_to_all | solution.py:85
  205.0 0.7 multiply_reduce_fusion.1
  205.7 0.7 reduce_sum.90
  206.4 4.9 %all-to-all-done.4 = f32[16,16,2]{1,2,0:T(2,128)S(1)} async-done(((f32[16,16,2]{1,2,0:T(2,128)}), f32[16,16,2]{1,2,0:T(2,128)S(1)}, u32[]{:S(2)}, u32[]{:S(2)}) %all-to-all-start.4) | async-done | bytes 2080 | tf_op jit(solution)/shard_map/all_to_all | solution.py:85
  211.3 0.6 reduce_sum.92
  (30 shorter events, 1.4 us)
Async XLA Ops:
  0.6 107.4 %copy-start = (bf16[1,128,6144]{2,1,0:T(8,128)(2,1)S(1)}, bf16[1,128,6144]{2,1,0:T(8,128)(2,1)}, u32[]{:S(2)}) copy-start(bf16[1,128,6144]{2,1,0:T(8,128)(2,1)} %param.12) | copy-start | bytes 4718596
  104.9 1.4 copy-start.1
  105.2 1.8 copy-start.2
  161.6 10.6 %copy-start.4 = (f32[16,2]{0,1:T(2,128)S(1)}, f32[16,2]{0,1:T(2,128)}, u32[]{:S(2)}) copy-start(f32[16,2]{0,1:T(2,128)} %param.9) | copy-start | bytes 388
  161.6 10.7 %copy-start.3 = (bf16[16,384]{1,0:T(8,128)(2,1)S(1)}, bf16[16,384]{1,0:T(8,128)(2,1)}, u32[]{:S(2)}) copy-start(bf16[16,384]{1,0:T(8,128)(2,1)} %param.13) | copy-start | bytes 36868
  165.2 35.0 %all-to-all-start.3 = ((bf16[32,5,768]{2,1,0:T(8,128)(2,1)}), bf16[32,5,768]{2,1,0:T(8,128)(2,1)S(1)}, u32[]{:S(2)}, u32[]{:S(2)}) async-start(bf16[32,5,768]{2,1,0:T(8,128)(2,1)} %reshape.82), calls=%async_computation.3 | async-start | bytes 786432 | tf_op jit(solution)/shard_map/all_to_all | solution.py:71
  201.5 9.9 %all-to-all-start.4 = ((f32[16,16,2]{1,2,0:T(2,128)}), f32[16,16,2]{1,2,0:T(2,128)S(1)}, u32[]{:S(2)}, u32[]{:S(2)}) async-start(f32[16,16,2]{1,2,0:T(2,128)} %broadcast_in_dim.28), calls=%async_computation.4 | async-start | bytes 32768 | tf_op jit(solution)/shard_map/all_to_all | solution.py:85

commit v4 on v3

--- a/solution.py
+++ b/solution.py
@@ -9,6 +9,7 @@
     feat = tokens.shape[1]
     top = expert_ids.shape[1]
     devices_all = lax.axis_size("expert")
+    planes = lax.axis_size("pipe") * lax.axis_size("tensor")
     experts = min(8, devices_all)
     group = devices_all // experts
     capacity = min(
@@ -16,6 +17,10 @@
         max(2, max(5 * tok_rows * top // (4 * experts), (tok_rows * top + experts - 1) // experts)),
     )
     slots = experts * capacity
+    rows_n = devices_all * capacity
+    core = lax.axis_index("expert") % 2
+    first_core = core == 0
+    partner = [(i, i ^ 1) for i in range(devices_all)]
     flat_ids = expert_ids.reshape(-1)
     onehot = (flat_ids[:, None] == jnp.arange(experts, dtype=jnp.int32)[None, :]).astype(jnp.int32)
     position = jnp.sum(jnp.cumsum(onehot, axis=0) * onehot, axis=1) - 1
@@ -28,15 +33,18 @@
     scaled = jnp.dot(
         select_gate, d_out.astype(jnp.float32), precision=lax.Precision.HIGHEST
     ).astype(jnp.bfloat16)
-    send = jnp.concatenate([picked, scaled], axis=1).reshape(experts, capacity, 2 * feat)
-    send = jnp.repeat(send, group, axis=0)
+    pair = jnp.stack(
+        [picked.reshape(experts, capacity, feat), scaled.reshape(experts, capacity, feat)], axis=1
+    )
+    send = jnp.concatenate([pair] * (group // 2), axis=1).reshape(devices_all, capacity, feat)
     recv = lax.all_to_all(send, "expert", split_axis=0, concat_axis=0, tiled=True)
-    recv = recv.reshape(devices_all * capacity, 2 * feat)
-    planes = lax.axis_size("pipe") * lax.axis_size("tensor")
+    recv = recv.reshape(rows_n, feat)
     spread = jnp.broadcast_to(recv[None], (planes,) + recv.shape)
     gathered = lax.all_to_all(spread, ("pipe", "tensor"), 0, 0, tiled=True)
-    rows_x = gathered[:, :, :feat].transpose(1, 0, 2).reshape(devices_all * capacity, planes * feat)
-    rows_dy = gathered[:, :, feat:].transpose(1, 0, 2).reshape(devices_all * capacity, planes * feat)
+    own_rows = gathered.transpose(1, 0, 2).reshape(rows_n, planes * feat)
+    other_rows = lax.ppermute(own_rows, "expert", partner)
+    rows_x = jnp.where(first_core, own_rows, other_rows)
+    rows_dy = jnp.where(first_core, other_rows, own_rows)
     gate_proj = w_gate[0]
     up_proj = w_up[0]
     down_proj = w_down[0]
@@ -45,7 +53,7 @@
     h_up = jnp.dot(rows_x, up_proj, preferred_element_type=jnp.float32)
     sig = jax.nn.sigmoid(h_gate)
     hidden = (h_gate * sig * h_up).astype(jnp.bfloat16)
-    out_terms = jnp.dot(hidden, down_proj, preferred_element_type=jnp.float32)
+    out_terms = jnp.dot(hidden, down_proj, preferred_element_type=jnp.float32).astype(jnp.bfloat16)
     d_hidden = lax.dot_general(
         rows_dy, down_proj, contract_last, preferred_element_type=jnp.float32
     )
@@ -57,23 +65,19 @@
     dx_terms = dx_terms + lax.dot_general(
         d_up_h, up_proj, contract_last, preferred_element_type=jnp.float32
     )
-    rows_n = devices_all * capacity
-    terms = jnp.concatenate(
-        [
-            out_terms.astype(jnp.bfloat16).reshape(rows_n, planes, feat),
-            dx_terms.astype(jnp.bfloat16).reshape(rows_n, planes, feat),
-        ],
-        axis=2,
-    ).transpose(1, 0, 2)
+    dx_terms = dx_terms.astype(jnp.bfloat16)
+    keep = jnp.where(first_core, out_terms, dx_terms)
+    give = jnp.where(first_core, dx_terms, out_terms)
+    got = lax.ppermute(give, "expert", partner)
+    both = (keep.astype(jnp.float32) + got.astype(jnp.float32)).astype(jnp.bfloat16)
+    terms = both.reshape(rows_n, planes, feat).transpose(1, 0, 2)
     reduced = lax.all_to_all(terms, ("pipe", "tensor"), 0, 0, tiled=True)
     shares = jnp.sum(reduced.astype(jnp.float32), axis=0).astype(jnp.bfloat16)
-    back_send = shares.reshape(devices_all, capacity, 2 * feat)
+    back_send = shares.reshape(devices_all, capacity, feat)
     back = lax.all_to_all(back_send, "expert", split_axis=0, concat_axis=0, tiled=True)
-    back_rows = (
-        jnp.sum(back.astype(jnp.float32).reshape(experts, group, capacity, 2 * feat), axis=1)
-        .astype(jnp.bfloat16)
-        .reshape(slots, 2 * feat)
-    )
+    back = back.astype(jnp.float32).reshape(experts, group // 2, 2, capacity, feat)
+    back_rows = jnp.sum(back, axis=1).astype(jnp.bfloat16)
+    back_rows = back_rows.transpose(0, 2, 1, 3).reshape(slots, 2 * feat)
     assign = picks.T.astype(jnp.bfloat16)
     a_both = jnp.dot(assign, back_rows, preferred_element_type=jnp.float32)
     a_out = a_both[:, :feat].reshape(tok_rows, top, feat)

time: 212 us -> 167 us (0.79)
  blocking collectives: 148 us -> 96.2 us
  starting transfers between devices: 10.5 us -> 15.2 us
  matrix products: 6.16 us -> 10.8 us
    all_to_all x1, blocking collectives: 53.9 us -> 31.8 us  [per_device(): gathered = lax.all_to_all(spread, ('pipe', 'tensor'), 0, 0, tiled=True)]
    all_to_all x1, blocking collectives: 49.9 us -> 29.2 us  [per_device(): reduced = lax.all_to_all(terms, ('pipe', 'tensor'), 0, 0, tiled=True)]
    all_to_all x1, blocking collectives: 44.5 us -> 35.2 us  [per_device(): lax.all_to_all(send, 'expert', split_axis=0, concat_axis=0, tiled=True)]
    all_to_all x1, waiting for transfers between devices: 27.8 us -> 18.7 us  [per_device(): lax.all_to_all(back_send, 'expert', split_axis=0, concat_axis=0, tiled=True)]
    ppermute x0 -> x2, waiting for transfers between devices: none -> 7.63 us  [the longest x1 3.94 us: per_device(): got = lax.ppermute(give, 'expert', partner)]
    ppermute x0 -> x2, starting transfers between devices: none -> 6.68 us  [the longest x1 4.76 us: per_device(): other_rows = lax.ppermute(own_rows, 'expert', partner)]
    dot_general x1, matrix products: 0.7 us -> 2.84 us  [per_device(): h_gate = jnp.dot(rows_x, gate_proj, preferred_element_type=jnp.float32)]
  transfers between devices with their start and end apart: 2 -> 4, of which waited for: 2 -> 4; matrix products, arithmetic and copies ran while one was open for 1% -> 1% of each run, Pallas kernels for 0% -> 0%
where the time goes in v4:
time: 167 us; the launch traced here: 166 us
  blocking collectives  96.2 us (58%)
  waiting for transfers between devices  31.3 us (19%)
  starting transfers between devices  15.2 us (9%)
  matrix products  10.8 us (6%)
  other arithmetic  6.36 us (4%)
  local copies, waits for them, and re-layouts  5.3 us (3%)
    all_to_all x1, blocking collectives, per_device(): lax.all_to_all(send, 'expert', split_axis=0, concat_axis=0, tiled=True)  35.2 us
    all_to_all x1, blocking collectives, per_device(): gathered = lax.all_to_all(spread, ('pipe', 'tensor'), 0, 0, tiled=True)  31.8 us
    all_to_all x1, blocking collectives, per_device(): reduced = lax.all_to_all(terms, ('pipe', 'tensor'), 0, 0, tiled=True)  29.2 us
    all_to_all x1, waiting for transfers between devices, per_device(): lax.all_to_all(back_send, 'expert', split_axis=0, concat_axis=0, tiled=True)  18.7 us
    all_to_all x1, starting transfers between devices, per_device(): lax.all_to_all(back_send, 'expert', split_axis=0, concat_axis=0, tiled=True)  4.99 us
    all_to_all x1, waiting for transfers between devices, per_device(): lax.all_to_all(dots_spread, ('pipe', 'tensor'), 0, 0, tiled=True)  4.94 us
    ppermute x1, starting transfers between devices, per_device(): other_rows = lax.ppermute(own_rows, 'expert', partner)  4.76 us
    ppermute x1, waiting for transfers between devices, per_device(): got = lax.ppermute(give, 'expert', partner)  3.94 us
  transfers between devices with their start and end apart: 4, of which 4 were waited for; matrix products, arithmetic and copies ran while one was open for 1% of the time, Pallas kernels for 0%

profile of v4, /device:TPU:1, one launch (start us, length us, event | category | flops | bytes accessed | tf_op | source)
XLA Modules:
  0.0 166.0 jit_solution(4559102972265169841)
XLA Ops:
  0.6 0.9 copy.45
  1.9 0.5 multiply_add_fusion.1
  2.6 0.7 multiply_add_fusion
  3.3 0.8 convert_reduce_fusion
  4.1 0.9 convolution_convert_fusion.2
  5.0 0.9 convolution_convert_fusion.1
  6.0 35.2 %all_to_all.25 = bf16[32,5,384]{2,1,0:T(8,128)(2,1)S(1)} all-to-all(bf16[32,5,384]{2,1,0:T(8,128)(2,1)S(1)} %bitcast.46), channel_id=1, replica_groups=mesh['pipe'=4,'expert'=32,'tensor'=4] {'expert'}, dimensions={0} | all-to-all | bytes 245760 | tf_op jit(solution)/shard_map/all_to_all | solution.py:40
  41.5 31.8 %all_to_all.26 = bf16[16,160,384]{2,1,0:T(8,128)(2,1)S(1)} all-to-all(bf16[16,160,384]{2,1,0:T(8,128)(2,1)S(1)} %broadcast_in_dim.9), channel_id=1, replica_groups=mesh['pipe'=4,'expert'=32,'tensor'=4] {'pipe','tensor'}, dimensions={0} | all-to-all | bytes 3932160 | tf_op jit(solution)/shard_map/all_to_all | solution.py:43
  73.6 4.8 %collective-permute-start = (bf16[160,6144]{1,0:T(8,128)(2,1)S(1)}, bf16[160,6144]{1,0:T(8,128)(2,1)}, u32[]{:S(2)}, u32[]{:S(2)}) collective-permute-start(bf16[160,6144]{1,0:T(8,128)(2,1)S(1)} %bitcast.41), channel_id=1, source_target_pairs={{0,4},{4,0},{8,12},{12,8},{16,20},{20,16},{24,28},{28,24},{32,36},... | collective-permute-start | bytes 5898248 | tf_op jit(solution)/shard_map/ppermute | solution.py:45
  78.4 3.7 %collective-permute-done = bf16[160,6144]{1,0:T(8,128)(2,1)} collective-permute-done((bf16[160,6144]{1,0:T(8,128)(2,1)S(1)}, bf16[160,6144]{1,0:T(8,128)(2,1)}, u32[]{:S(2)}, u32[]{:S(2)}) %collective-permute-start) | collective-permute-done | bytes 1966112 | tf_op jit(solution)/shard_map/ppermute | solution.py:45
  82.1 2.8 %fusion.11 = f32[160,128]{1,0:T(8,128)S(1)} fusion(bf16[1,6144,128]{2,1,0:T(8,128)(2,1)} %param.10, bf16[160,6144]{1,0:T(8,128)(2,1)S(1)} %bitcast.42, bf16[160,6144]{1,0:T(8,128)(2,1)} %collective-permute-done, pred[]{:T(512)S(6)} %eq.45), kind=kOutput, calls=%fused_computation.17 | convolution fusion | flops 252641280 | bytes 5586945 | tf_op jit(solution)/shard_map/dot_general | solution.py:52
  85.0 2.5 %fusion.7 = f32[160,128]{1,0:T(8,128)S(1)} fusion(bf16[1,6144,128]{2,1,0:T(8,128)(2,1)S(1)} %copy-done, bf16[160,6144]{1,0:T(8,128)(2,1)S(1)} %bitcast.43, bf16[160,6144]{1,0:T(8,128)(2,1)} %collective-permute-done, pred[]{:T(512)S(6)} %eq.45), kind=kOutput, calls=%fused_computation.13 | convolution fusion | flops 252641280 | bytes 5586945 | tf_op jit(solution)/shard_map/dot_general | solution.py:53
  87.5 0.7 convolution_convert_fusion
  88.2 0.7 fusion.1
  88.9 0.7 copy-done.2
  89.6 0.7 fusion.9
  90.3 0.7 broadcast_select_fusion
  91.0 1.9 %collective-permute-start.1 = (bf16[160,6144]{1,0:T(8,128)(2,1)S(1)}, bf16[160,6144]{1,0:T(8,128)(2,1)S(1)}, u32[]{:S(2)}, u32[]{:S(2)}) collective-permute-start(bf16[160,6144]{1,0:T(8,128)(2,1)S(1)} %get-tuple-element.10), channel_id=1, source_target_pairs={{0,4},{4,0},{8,12},{12,8},{16,20},{20,16},{24,28},{28,24},{32,36},... | collective-permute-start | bytes 5898248 | tf_op jit(solution)/shard_map/ppermute | solution.py:71
  92.9 3.9 %collective-permute-done.1 = bf16[160,6144]{1,0:T(8,128)(2,1)S(1)} collective-permute-done((bf16[160,6144]{1,0:T(8,128)(2,1)S(1)}, bf16[160,6144]{1,0:T(8,128)(2,1)S(1)}, u32[]{:S(2)}, u32[]{:S(2)}) %collective-permute-start.1) | collective-permute-done | bytes 1966112 | tf_op jit(solution)/shard_map/ppermute | solution.py:71
  96.8 0.9 add_convert_fusion
  98.0 29.2 %all_to_all.27 = bf16[16,160,384]{2,1,0:T(8,128)(2,1)S(1)} all-to-all(bf16[16,160,384]{2,1,0:T(8,128)(2,1)S(1)} %bitcast.39), channel_id=1, replica_groups=mesh['pipe'=4,'expert'=32,'tensor'=4] {'pipe','tensor'}, dimensions={0} | all-to-all | bytes 3932160 | tf_op jit(solution)/shard_map/all_to_all | solution.py:74
  127.2 0.9 reduce_sum.87
  128.1 1.6 reshape.70
  129.7 5.0 %all-to-all-start.3 = ((bf16[32,5,384]{2,1,0:T(8,128)(2,1)}), bf16[32,5,384]{2,1,0:T(8,128)(2,1)S(1)}, u32[]{:S(2)}, u32[]{:S(2)}) async-start(bf16[32,5,384]{2,1,0:T(8,128)(2,1)} %reshape.70), calls=%async_computation.3 | async-start | bytes 393216 | tf_op jit(solution)/shard_map/all_to_all | solution.py:77
  134.9 18.7 %all-to-all-done.3 = bf16[32,5,384]{2,1,0:T(8,128)(2,1)S(1)} async-done(((bf16[32,5,384]{2,1,0:T(8,128)(2,1)}), bf16[32,5,384]{2,1,0:T(8,128)(2,1)S(1)}, u32[]{:S(2)}, u32[]{:S(2)}) %all-to-all-start.3) | async-done | bytes 122912 | tf_op jit(solution)/shard_map/all_to_all | solution.py:77
  153.7 0.9 fusion.17
  154.9 0.6 broadcast_in_dim.11
  155.5 3.5 %all-to-all-start.4 = ((f32[16,16,2]{1,2,0:T(2,128)}), f32[16,16,2]{1,2,0:T(2,128)S(1)}, u32[]{:S(2)}, u32[]{:S(2)}) async-start(f32[16,16,2]{1,2,0:T(2,128)} %broadcast_in_dim.11), calls=%async_computation.4 | async-start | bytes 32768 | tf_op jit(solution)/shard_map/all_to_all | solution.py:89
  159.0 0.7 multiply_reduce_fusion.1
  159.8 0.7 reduce_sum.90
  160.4 4.9 %all-to-all-done.4 = f32[16,16,2]{1,2,0:T(2,128)S(1)} async-done(((f32[16,16,2]{1,2,0:T(2,128)}), f32[16,16,2]{1,2,0:T(2,128)S(1)}, u32[]{:S(2)}, u32[]{:S(2)}) %all-to-all-start.4) | async-done | bytes 2080 | tf_op jit(solution)/shard_map/all_to_all | solution.py:89
  165.4 0.6 reduce_sum.92
  (34 shorter events, 2.0 us)
Async XLA Ops:
  0.6 84.3 %copy-start = (bf16[1,6144,128]{2,1,0:T(8,128)(2,1)S(1)}, bf16[1,6144,128]{2,1,0:T(8,128)(2,1)}, u32[]{:S(2)}) copy-start(bf16[1,6144,128]{2,1,0:T(8,128)(2,1)} %param.11) | copy-start | bytes 4718596
  73.6 8.5 %collective-permute-start = (bf16[160,6144]{1,0:T(8,128)(2,1)S(1)}, bf16[160,6144]{1,0:T(8,128)(2,1)}, u32[]{:S(2)}, u32[]{:S(2)}) collective-permute-start(bf16[160,6144]{1,0:T(8,128)(2,1)S(1)} %bitcast.41), channel_id=1, source_target_pairs={{0,4},{4,0},{8,12},{12,8},{16,20},{20,16},{24,28},{28,24},{32,36},... | collective-permute-start | bytes 5898248 | tf_op jit(solution)/shard_map/ppermute | solution.py:45
  84.9 2.5 %copy-start.1 = (bf16[1,128,6144]{2,1,0:T(8,128)(2,1)S(1)}, bf16[1,128,6144]{2,1,0:T(8,128)(2,1)}, u32[]{:S(2)}) copy-start(bf16[1,128,6144]{2,1,0:T(8,128)(2,1)} %param.12) | copy-start | bytes 4718596
  88.2 1.4 copy-start.2
  91.0 5.9 %collective-permute-start.1 = (bf16[160,6144]{1,0:T(8,128)(2,1)S(1)}, bf16[160,6144]{1,0:T(8,128)(2,1)S(1)}, u32[]{:S(2)}, u32[]{:S(2)}) collective-permute-start(bf16[160,6144]{1,0:T(8,128)(2,1)S(1)} %get-tuple-element.10), channel_id=1, source_target_pairs={{0,4},{4,0},{8,12},{12,8},{16,20},{20,16},{24,28},{28,24},{32,36},... | collective-permute-start | bytes 5898248 | tf_op jit(solution)/shard_map/ppermute | solution.py:71
  127.2 7.6 %copy-start.4 = (f32[16,2]{0,1:T(2,128)S(1)}, f32[16,2]{0,1:T(2,128)}, u32[]{:S(2)}) copy-start(f32[16,2]{0,1:T(2,128)} %param.9) | copy-start | bytes 388
  127.2 7.7 %copy-start.3 = (bf16[16,384]{1,0:T(8,128)(2,1)S(1)}, bf16[16,384]{1,0:T(8,128)(2,1)}, u32[]{:S(2)}) copy-start(bf16[16,384]{1,0:T(8,128)(2,1)} %param.13) | copy-start | bytes 36868
  129.7 23.8 %all-to-all-start.3 = ((bf16[32,5,384]{2,1,0:T(8,128)(2,1)}), bf16[32,5,384]{2,1,0:T(8,128)(2,1)S(1)}, u32[]{:S(2)}, u32[]{:S(2)}) async-start(bf16[32,5,384]{2,1,0:T(8,128)(2,1)} %reshape.70), calls=%async_computation.3 | async-start | bytes 393216 | tf_op jit(solution)/shard_map/all_to_all | solution.py:77
  155.5 9.9 %all-to-all-start.4 = ((f32[16,16,2]{1,2,0:T(2,128)}), f32[16,16,2]{1,2,0:T(2,128)S(1)}, u32[]{:S(2)}, u32[]{:S(2)}) async-start(f32[16,16,2]{1,2,0:T(2,128)} %broadcast_in_dim.11), calls=%async_computation.4 | async-start | bytes 32768 | tf_op jit(solution)/shard_map/all_to_all | solution.py:89

commit v5 on v4

--- a/solution.py
+++ b/solution.py
@@ -28,11 +28,11 @@
     picks = (jnp.arange(slots, dtype=jnp.int32)[:, None] == slot_of[None, :]).astype(jnp.float32)
     pick_rows = picks.reshape(slots, tok_rows, top)
     select_tok = jnp.sum(pick_rows, axis=2).astype(jnp.bfloat16)
-    select_gate = jnp.sum(pick_rows * gates[None, :, :], axis=2)
-    picked = jnp.dot(select_tok, tokens, preferred_element_type=jnp.float32).astype(jnp.bfloat16)
-    scaled = jnp.dot(
-        select_gate, d_out.astype(jnp.float32), precision=lax.Precision.HIGHEST
-    ).astype(jnp.bfloat16)
+    slot_gate = jnp.sum(pick_rows * gates[None, :, :], axis=(1, 2))
+    both_in = jnp.concatenate([tokens, d_out], axis=1)
+    chosen = jnp.dot(select_tok, both_in, preferred_element_type=jnp.float32)
+    picked = chosen[:, :feat].astype(jnp.bfloat16)
+    scaled = (chosen[:, feat:] * slot_gate[:, None]).astype(jnp.bfloat16)
     pair = jnp.stack(
         [picked.reshape(experts, capacity, feat), scaled.reshape(experts, capacity, feat)], axis=1
     )

time: 167 us -> 166 us (level)
  no operation moved by 1% of the time
where the time goes in v5:
time: 166 us; the launch traced here: 165 us
  blocking collectives  96.2 us (58%)
  waiting for transfers between devices  31.3 us (19%)
  starting transfers between devices  15.2 us (9%)
  matrix products  9.9 us (6%)
  other arithmetic  6.45 us (4%)
  local copies, waits for them, and re-layouts  5.31 us (3%)
    all_to_all x1, blocking collectives, per_device(): lax.all_to_all(send, 'expert', split_axis=0, concat_axis=0, tiled=True)  35.2 us
    all_to_all x1, blocking collectives, per_device(): gathered = lax.all_to_all(spread, ('pipe', 'tensor'), 0, 0, tiled=True)  31.8 us
    all_to_all x1, blocking collectives, per_device(): reduced = lax.all_to_all(terms, ('pipe', 'tensor'), 0, 0, tiled=True)  29.2 us
    all_to_all x1, waiting for transfers between devices, per_device(): lax.all_to_all(back_send, 'expert', split_axis=0, concat_axis=0, tiled=True)  18.7 us
    all_to_all x1, starting transfers between devices, per_device(): lax.all_to_all(back_send, 'expert', split_axis=0, concat_axis=0, tiled=True)  5.01 us
    all_to_all x1, waiting for transfers between devices, per_device(): lax.all_to_all(dots_spread, ('pipe', 'tensor'), 0, 0, tiled=True)  4.94 us
    ppermute x1, starting transfers between devices, per_device(): other_rows = lax.ppermute(own_rows, 'expert', partner)  4.76 us
    ppermute x1, waiting for transfers between devices, per_device(): got = lax.ppermute(give, 'expert', partner)  3.94 us
  transfers between devices with their start and end apart: 4, of which 4 were waited for; matrix products, arithmetic and copies ran while one was open for 1% of the time, Pallas kernels for 0%

profile of v5, /device:TPU:1, one launch (start us, length us, event | category | flops | bytes accessed | tf_op | source)
XLA Modules:
  0.0 165.2 jit_solution(13053758321963169801)
XLA Ops:
  0.6 0.9 copy.45
  1.9 0.5 multiply_add_fusion.1
  2.6 0.7 multiply_add_fusion
  3.3 0.8 select_reduce_fusion
  4.1 0.9 fusion.17
  5.2 35.2 %all_to_all.25 = bf16[32,5,384]{2,1,0:T(8,128)(2,1)S(1)} all-to-all(bf16[32,5,384]{2,1,0:T(8,128)(2,1)S(1)} %bitcast.43), channel_id=1, replica_groups=mesh['pipe'=4,'expert'=32,'tensor'=4] {'expert'}, dimensions={0} | all-to-all | bytes 245760 | tf_op jit(solution)/shard_map/all_to_all | solution.py:40
  40.6 31.8 %all_to_all.26 = bf16[16,160,384]{2,1,0:T(8,128)(2,1)S(1)} all-to-all(bf16[16,160,384]{2,1,0:T(8,128)(2,1)S(1)} %broadcast_in_dim.9), channel_id=1, replica_groups=mesh['pipe'=4,'expert'=32,'tensor'=4] {'pipe','tensor'}, dimensions={0} | all-to-all | bytes 3932160 | tf_op jit(solution)/shard_map/all_to_all | solution.py:43
  72.5 0.3 copy.56
  72.8 4.8 %collective-permute-start = (bf16[160,6144]{1,0:T(8,128)(2,1)S(1)}, bf16[160,6144]{1,0:T(8,128)(2,1)}, u32[]{:S(2)}, u32[]{:S(2)}) collective-permute-start(bf16[160,6144]{1,0:T(8,128)(2,1)S(1)} %bitcast.38), channel_id=1, source_target_pairs={{0,4},{4,0},{8,12},{12,8},{16,20},{20,16},{24,28},{28,24},{32,36},... | collective-permute-start | bytes 5898248 | tf_op jit(solution)/shard_map/ppermute | solution.py:45
  77.6 3.7 %collective-permute-done = bf16[160,6144]{1,0:T(8,128)(2,1)} collective-permute-done((bf16[160,6144]{1,0:T(8,128)(2,1)S(1)}, bf16[160,6144]{1,0:T(8,128)(2,1)}, u32[]{:S(2)}, u32[]{:S(2)}) %collective-permute-start) | collective-permute-done | bytes 1966112 | tf_op jit(solution)/shard_map/ppermute | solution.py:45
  81.3 2.8 %fusion.11 = f32[160,128]{1,0:T(8,128)S(1)} fusion(bf16[1,6144,128]{2,1,0:T(8,128)(2,1)} %param.10, bf16[160,6144]{1,0:T(8,128)(2,1)S(1)} %bitcast.39, bf16[160,6144]{1,0:T(8,128)(2,1)} %collective-permute-done, pred[]{:T(512)S(6)} %eq.45), kind=kOutput, calls=%fused_computation.17 | convolution fusion | flops 252641280 | bytes 5586945 | tf_op jit(solution)/shard_map/dot_general | solution.py:52
  84.1 2.5 %fusion.7 = f32[160,128]{1,0:T(8,128)S(1)} fusion(bf16[1,6144,128]{2,1,0:T(8,128)(2,1)S(1)} %copy-done, bf16[160,6144]{1,0:T(8,128)(2,1)S(1)} %bitcast.40, bf16[160,6144]{1,0:T(8,128)(2,1)} %collective-permute-done, pred[]{:T(512)S(6)} %eq.45), kind=kOutput, calls=%fused_computation.13 | convolution fusion | flops 252641280 | bytes 5586945 | tf_op jit(solution)/shard_map/dot_general | solution.py:53
  86.7 0.7 convolution_convert_fusion
  87.4 0.7 fusion.1
  88.1 0.7 copy-done.2
  88.8 0.7 fusion.9
  89.4 0.7 broadcast_select_fusion
  90.2 1.9 %collective-permute-start.1 = (bf16[160,6144]{1,0:T(8,128)(2,1)S(1)}, bf16[160,6144]{1,0:T(8,128)(2,1)S(1)}, u32[]{:S(2)}, u32[]{:S(2)}) collective-permute-start(bf16[160,6144]{1,0:T(8,128)(2,1)S(1)} %get-tuple-element.10), channel_id=1, source_target_pairs={{0,4},{4,0},{8,12},{12,8},{16,20},{20,16},{24,28},{28,24},{32,36},... | collective-permute-start | bytes 5898248 | tf_op jit(solution)/shard_map/ppermute | solution.py:71
  92.1 3.9 %collective-permute-done.1 = bf16[160,6144]{1,0:T(8,128)(2,1)S(1)} collective-permute-done((bf16[160,6144]{1,0:T(8,128)(2,1)S(1)}, bf16[160,6144]{1,0:T(8,128)(2,1)S(1)}, u32[]{:S(2)}, u32[]{:S(2)}) %collective-permute-start.1) | collective-permute-done | bytes 1966112 | tf_op jit(solution)/shard_map/ppermute | solution.py:71
  96.0 0.9 add_convert_fusion
  97.2 29.2 %all_to_all.27 = bf16[16,160,384]{2,1,0:T(8,128)(2,1)S(1)} all-to-all(bf16[16,160,384]{2,1,0:T(8,128)(2,1)S(1)} %bitcast.36), channel_id=1, replica_groups=mesh['pipe'=4,'expert'=32,'tensor'=4] {'pipe','tensor'}, dimensions={0} | all-to-all | bytes 3932160 | tf_op jit(solution)/shard_map/all_to_all | solution.py:74
  126.3 0.9 reduce_sum.87
  127.3 1.6 reshape.71
  128.9 5.0 %all-to-all-start.3 = ((bf16[32,5,384]{2,1,0:T(8,128)(2,1)}), bf16[32,5,384]{2,1,0:T(8,128)(2,1)S(1)}, u32[]{:S(2)}, u32[]{:S(2)}) async-start(bf16[32,5,384]{2,1,0:T(8,128)(2,1)} %reshape.71), calls=%async_computation.3 | async-start | bytes 393216 | tf_op jit(solution)/shard_map/all_to_all | solution.py:77
  134.1 18.7 %all-to-all-done.3 = bf16[32,5,384]{2,1,0:T(8,128)(2,1)S(1)} async-done(((bf16[32,5,384]{2,1,0:T(8,128)(2,1)}), bf16[32,5,384]{2,1,0:T(8,128)(2,1)S(1)}, u32[]{:S(2)}, u32[]{:S(2)}) %all-to-all-start.3) | async-done | bytes 122912 | tf_op jit(solution)/shard_map/all_to_all | solution.py:77
  152.9 0.9 fusion.22
  154.1 0.6 broadcast_in_dim.11
  154.7 3.5 %all-to-all-start.4 = ((f32[16,16,2]{1,2,0:T(2,128)}), f32[16,16,2]{1,2,0:T(2,128)S(1)}, u32[]{:S(2)}, u32[]{:S(2)}) async-start(f32[16,16,2]{1,2,0:T(2,128)} %broadcast_in_dim.11), calls=%async_computation.4 | async-start | bytes 32768 | tf_op jit(solution)/shard_map/all_to_all | solution.py:89
  158.2 0.7 multiply_reduce_fusion.1
  159.0 0.7 reduce_sum.90
  159.6 4.9 %all-to-all-done.4 = f32[16,16,2]{1,2,0:T(2,128)S(1)} async-done(((f32[16,16,2]{1,2,0:T(2,128)}), f32[16,16,2]{1,2,0:T(2,128)S(1)}, u32[]{:S(2)}, u32[]{:S(2)}) %all-to-all-start.4) | async-done | bytes 2080 | tf_op jit(solution)/shard_map/all_to_all | solution.py:89
  164.6 0.6 reduce_sum.92
  (35 shorter events, 1.8 us)
Async XLA Ops:
  0.6 83.5 %copy-start = (bf16[1,6144,128]{2,1,0:T(8,128)(2,1)S(1)}, bf16[1,6144,128]{2,1,0:T(8,128)(2,1)}, u32[]{:S(2)}) copy-start(bf16[1,6144,128]{2,1,0:T(8,128)(2,1)} %param.11) | copy-start | bytes 4718596
  72.8 8.5 %collective-permute-start = (bf16[160,6144]{1,0:T(8,128)(2,1)S(1)}, bf16[160,6144]{1,0:T(8,128)(2,1)}, u32[]{:S(2)}, u32[]{:S(2)}) collective-permute-start(bf16[160,6144]{1,0:T(8,128)(2,1)S(1)} %bitcast.38), channel_id=1, source_target_pairs={{0,4},{4,0},{8,12},{12,8},{16,20},{20,16},{24,28},{28,24},{32,36},... | collective-permute-start | bytes 5898248 | tf_op jit(solution)/shard_map/ppermute | solution.py:45
  84.1 2.5 %copy-start.1 = (bf16[1,128,6144]{2,1,0:T(8,128)(2,1)S(1)}, bf16[1,128,6144]{2,1,0:T(8,128)(2,1)}, u32[]{:S(2)}) copy-start(bf16[1,128,6144]{2,1,0:T(8,128)(2,1)} %param.12) | copy-start | bytes 4718596
  87.3 1.4 copy-start.2
  90.2 5.9 %collective-permute-start.1 = (bf16[160,6144]{1,0:T(8,128)(2,1)S(1)}, bf16[160,6144]{1,0:T(8,128)(2,1)S(1)}, u32[]{:S(2)}, u32[]{:S(2)}) collective-permute-start(bf16[160,6144]{1,0:T(8,128)(2,1)S(1)} %get-tuple-element.10), channel_id=1, source_target_pairs={{0,4},{4,0},{8,12},{12,8},{16,20},{20,16},{24,28},{28,24},{32,36},... | collective-permute-start | bytes 5898248 | tf_op jit(solution)/shard_map/ppermute | solution.py:71
  126.3 7.6 %copy-start.4 = (f32[16,2]{0,1:T(2,128)S(1)}, f32[16,2]{0,1:T(2,128)}, u32[]{:S(2)}) copy-start(f32[16,2]{0,1:T(2,128)} %param.9) | copy-start | bytes 388
  126.3 7.7 %copy-start.3 = (bf16[16,384]{1,0:T(8,128)(2,1)S(1)}, bf16[16,384]{1,0:T(8,128)(2,1)}, u32[]{:S(2)}) copy-start(bf16[16,384]{1,0:T(8,128)(2,1)} %param.13) | copy-start | bytes 36868
  128.9 23.9 %all-to-all-start.3 = ((bf16[32,5,384]{2,1,0:T(8,128)(2,1)}), bf16[32,5,384]{2,1,0:T(8,128)(2,1)S(1)}, u32[]{:S(2)}, u32[]{:S(2)}) async-start(bf16[32,5,384]{2,1,0:T(8,128)(2,1)} %reshape.71), calls=%async_computation.3 | async-start | bytes 393216 | tf_op jit(solution)/shard_map/all_to_all | solution.py:77
  154.7 9.9 %all-to-all-start.4 = ((f32[16,16,2]{1,2,0:T(2,128)}), f32[16,16,2]{1,2,0:T(2,128)S(1)}, u32[]{:S(2)}, u32[]{:S(2)}) async-start(f32[16,16,2]{1,2,0:T(2,128)} %broadcast_in_dim.11), calls=%async_computation.4 | async-start | bytes 32768 | tf_op jit(solution)/shard_map/all_to_all | solution.py:89

commit v6 on v5

--- a/solution.py
+++ b/solution.py
@@ -69,24 +69,45 @@
     keep = jnp.where(first_core, out_terms, dx_terms)
     give = jnp.where(first_core, dx_terms, out_terms)
     got = lax.ppermute(give, "expert", partner)
-    both = (keep.astype(jnp.float32) + got.astype(jnp.float32)).astype(jnp.bfloat16)
+    both_f32 = keep.astype(jnp.float32) + got.astype(jnp.float32)
+    both = both_f32.astype(jnp.bfloat16)
+    row_dots = jnp.sum(rows_dy.astype(jnp.float32) * both_f32, axis=1)
+    dots_hi = row_dots.astype(jnp.bfloat16)
+    dots_lo = (row_dots - dots_hi.astype(jnp.float32)).astype(jnp.bfloat16)
+    dots_row = jnp.concatenate(
+        [dots_hi, dots_lo, jnp.zeros((feat - 2 * rows_n,), jnp.bfloat16)]
+    ).reshape(1, 1, feat)
     terms = both.reshape(rows_n, planes, feat).transpose(1, 0, 2)
-    reduced = lax.all_to_all(terms, ("pipe", "tensor"), 0, 0, tiled=True)
-    shares = jnp.sum(reduced.astype(jnp.float32), axis=0).astype(jnp.bfloat16)
-    back_send = shares.reshape(devices_all, capacity, feat)
+    terms = jnp.concatenate([terms, jnp.broadcast_to(dots_row, (planes, 1, feat))], axis=1)
+    reduced = lax.all_to_all(terms, ("pipe", "tensor"), 0, 0, tiled=True).astype(jnp.float32)
+    shares = jnp.sum(reduced[:, :rows_n], axis=0).astype(jnp.bfloat16)
+    dots_sum = jnp.sum(reduced[:, rows_n, :rows_n] + reduced[:, rows_n, rows_n:2 * rows_n], axis=0)
+    back_hi = dots_sum.astype(jnp.bfloat16)
+    back_lo = (dots_sum - back_hi.astype(jnp.float32)).astype(jnp.bfloat16)
+    back_dots = jnp.concatenate(
+        [
+            back_hi.reshape(devices_all, capacity),
+            back_lo.reshape(devices_all, capacity),
+            jnp.zeros((devices_all, feat - 2 * capacity), jnp.bfloat16),
+        ],
+        axis=1,
+    ).reshape(devices_all, 1, feat)
+    back_send = jnp.concatenate([shares.reshape(devices_all, capacity, feat), back_dots], axis=1)
     back = lax.all_to_all(back_send, "expert", split_axis=0, concat_axis=0, tiled=True)
-    back = back.astype(jnp.float32).reshape(experts, group // 2, 2, capacity, feat)
-    back_rows = jnp.sum(back, axis=1).astype(jnp.bfloat16)
+    back = back.astype(jnp.float32).reshape(experts, group // 2, 2, capacity + 1, feat)
+    back_rows = jnp.sum(back[:, :, :, :capacity], axis=1).astype(jnp.bfloat16)
     back_rows = back_rows.transpose(0, 2, 1, 3).reshape(slots, 2 * feat)
+    slot_dots = jnp.sum(
+        back[:, :, 0, capacity, :capacity] + back[:, :, 0, capacity, capacity:2 * capacity], axis=1
+    ).reshape(slots)
     assign = picks.T.astype(jnp.bfloat16)
     a_both = jnp.dot(assign, back_rows, preferred_element_type=jnp.float32)
     a_out = a_both[:, :feat].reshape(tok_rows, top, feat)
     a_dx = a_both[:, feat:].reshape(tok_rows, top, feat)
     moe_out = jnp.sum(gates[:, :, None] * a_out, axis=1).astype(jnp.bfloat16)
     grad_tokens = jnp.sum(a_dx, axis=1).astype(jnp.bfloat16)
-    partial_dots = jnp.sum(d_out.astype(jnp.float32)[:, None, :] * a_out, axis=2)
-    dots_spread = jnp.broadcast_to(partial_dots[None], (planes,) + partial_dots.shape)
-    grad_gates = jnp.sum(lax.all_to_all(dots_spread, ("pipe", "tensor"), 0, 0, tiled=True), axis=0)
+    assign_dots = jnp.sum(picks.T * slot_dots[None, :], axis=1).reshape(tok_rows, top)
+    grad_gates = assign_dots / gates
     return (moe_out, grad_tokens, grad_gates)
 
 

time: 166 us -> 164 us (0.988)
  blocking collectives: 96.2 us -> 67 us
  waiting for transfers between devices: 31.3 us -> 54 us
  other arithmetic: 6.45 us -> 10 us
  starting transfers between devices: 15.2 us -> 18.2 us
    all_to_all x1 -> x0, blocking collectives: 29.2 us -> none  [per_device(): reduced = lax.all_to_all(terms, ('pipe', 'tensor'), 0, 0, tiled=True)]
    all_to_all x1, waiting for transfers between devices: 4.94 us -> 27.7 us  [per_device(): lax.all_to_all(terms, ('pipe', 'tensor'), 0, 0, tiled=True)]
    convert_element_type x1 -> x4, other arithmetic: 0.94 us -> 3.63 us  [the longest x1 1.85 us: per_device(): lax.all_to_all(terms, ('pipe', 'tensor'), 0, 0, tiled=True)]
    concatenate x0 -> x3, other arithmetic: none -> 2.35 us  [the longest x1 1.5 us: per_device(): jnp.concatenate([terms, jnp.broadcast_to(dots_row, (planes, 1, feat))], a...]
    all_to_all x1, starting transfers between devices: 5.01 us -> 7.08 us  [per_device(): lax.all_to_all(back_send, 'expert', split_axis=0, concat_axis=0, tiled=True)]
  transfers between devices with their start and end apart: 4 -> 4, of which waited for: 4 -> 4; matrix products, arithmetic and copies ran while one was open for 1% -> 0% of each run, Pallas kernels for 0% -> 0%
where the time goes in v6:
time: 164 us; the launch traced here: 163 us
  blocking collectives  67 us (41%)
  waiting for transfers between devices  54 us (33%)
  starting transfers between devices  18.2 us (11%)
  other arithmetic  10 us (6%)
  matrix products  9.29 us (6%)
  local copies, waits for them, and re-layouts  3.97 us (2%)
    all_to_all x1, blocking collectives, per_device(): lax.all_to_all(send, 'expert', split_axis=0, concat_axis=0, tiled=True)  35.2 us
    all_to_all x1, blocking collectives, per_device(): gathered = lax.all_to_all(spread, ('pipe', 'tensor'), 0, 0, tiled=True)  31.8 us
    all_to_all x1, waiting for transfers between devices, per_device(): lax.all_to_all(terms, ('pipe', 'tensor'), 0, 0, tiled=True)  27.7 us
    all_to_all x1, waiting for transfers between devices, per_device(): lax.all_to_all(back_send, 'expert', split_axis=0, concat_axis=0, tiled=True)  18.8 us
    all_to_all x1, starting transfers between devices, per_device(): lax.all_to_all(back_send, 'expert', split_axis=0, concat_axis=0, tiled=True)  7.08 us
    ppermute x1, starting transfers between devices, per_device(): other_rows = lax.ppermute(own_rows, 'expert', partner)  4.76 us
    all_to_all x1, starting transfers between devices, per_device(): lax.all_to_all(terms, ('pipe', 'tensor'), 0, 0, tiled=True)  4.42 us
    ppermute x1, waiting for transfers between devices, per_device(): got = lax.ppermute(give, 'expert', partner)  3.94 us
  transfers between devices with their start and end apart: 4, of which 4 were waited for; matrix products, arithmetic and copies ran while one was open for 0% of the time, Pallas kernels for 0%

profile of v6, /device:TPU:1, one launch (start us, length us, event | category | flops | bytes accessed | tf_op | source)
XLA Modules:
  0.0 163.5 jit_solution(6568011197144005993)
XLA Ops:
  0.6 0.9 copy.54
  1.7 0.2 select_reduce_fusion.2
  2.1 0.7 multiply_add_fusion
  2.8 0.8 select_reduce_fusion.1
  3.6 0.9 fusion.16
  4.7 35.2 %all_to_all.20 = bf16[32,5,384]{2,1,0:T(8,128)(2,1)S(1)} all-to-all(bf16[32,5,384]{2,1,0:T(8,128)(2,1)S(1)} %bitcast.49), channel_id=1, replica_groups=mesh['pipe'=4,'expert'=32,'tensor'=4] {'expert'}, dimensions={0} | all-to-all | bytes 245760 | tf_op jit(solution)/shard_map/all_to_all | solution.py:40
  40.1 31.8 %all_to_all.21 = bf16[16,160,384]{2,1,0:T(8,128)(2,1)S(1)} all-to-all(bf16[16,160,384]{2,1,0:T(8,128)(2,1)S(1)} %broadcast_in_dim.11), channel_id=1, replica_groups=mesh['pipe'=4,'expert'=32,'tensor'=4] {'pipe','tensor'}, dimensions={0} | all-to-all | bytes 3932160 | tf_op jit(solution)/shard_map/all_to_all | solution.py:43
  72.0 0.3 copy.67
  72.3 4.8 %collective-permute-start = (bf16[160,6144]{1,0:T(8,128)(2,1)S(1)}, bf16[160,6144]{1,0:T(8,128)(2,1)}, u32[]{:S(2)}, u32[]{:S(2)}) collective-permute-start(bf16[160,6144]{1,0:T(8,128)(2,1)S(1)} %bitcast.41), channel_id=1, source_target_pairs={{0,4},{4,0},{8,12},{12,8},{16,20},{20,16},{24,28},{28,24},{32,36},... | collective-permute-start | bytes 5898248 | tf_op jit(solution)/shard_map/ppermute | solution.py:45
  77.1 3.7 %collective-permute-done = bf16[160,6144]{1,0:T(8,128)(2,1)} collective-permute-done((bf16[160,6144]{1,0:T(8,128)(2,1)S(1)}, bf16[160,6144]{1,0:T(8,128)(2,1)}, u32[]{:S(2)}, u32[]{:S(2)}) %collective-permute-start) | collective-permute-done | bytes 1966112 | tf_op jit(solution)/shard_map/ppermute | solution.py:45
  80.8 2.9 %fusion.10 = f32[160,128]{1,0:T(8,128)S(1)} fusion(bf16[1,6144,128]{2,1,0:T(8,128)(2,1)} %param.10, bf16[160,6144]{1,0:T(8,128)(2,1)S(1)} %bitcast.42, bf16[160,6144]{1,0:T(8,128)(2,1)} %collective-permute-done, pred[]{:T(512)S(6)} %eq.45), kind=kOutput, calls=%fused_computation.21 | convolution fusion | flops 252641280 | bytes 5586945 | tf_op jit(solution)/shard_map/dot_general | solution.py:52
  83.6 2.5 %fusion.6 = f32[160,128]{1,0:T(8,128)S(1)} fusion(bf16[1,6144,128]{2,1,0:T(8,128)(2,1)S(1)} %copy-done, bf16[160,6144]{1,0:T(8,128)(2,1)S(1)} %bitcast.43, bf16[160,6144]{1,0:T(8,128)(2,1)} %collective-permute-done, pred[]{:T(512)S(6)} %eq.45), kind=kOutput, calls=%fused_computation.17 | convolution fusion | flops 252641280 | bytes 5586945 | tf_op jit(solution)/shard_map/dot_general | solution.py:53
  86.2 0.7 convolution_convert_fusion
  86.9 0.7 fusion.2
  87.6 0.7 copy-done.2
  88.3 0.7 fusion.8
  88.9 0.8 broadcast_select_fusion
  89.7 1.9 %collective-permute-start.1 = (bf16[160,6144]{1,0:T(8,128)(2,1)S(1)}, bf16[160,6144]{1,0:T(8,128)(2,1)S(1)}, u32[]{:S(2)}, u32[]{:S(2)}) collective-permute-start(bf16[160,6144]{1,0:T(8,128)(2,1)S(1)} %get-tuple-element.30), channel_id=1, source_target_pairs={{0,4},{4,0},{8,12},{12,8},{16,20},{20,16},{24,28},{28,24},{32,36},... | collective-permute-start | bytes 5898248 | tf_op jit(solution)/shard_map/ppermute | solution.py:71
  91.6 3.9 %collective-permute-done.1 = bf16[160,6144]{1,0:T(8,128)(2,1)S(1)} collective-permute-done((bf16[160,6144]{1,0:T(8,128)(2,1)S(1)}, bf16[160,6144]{1,0:T(8,128)(2,1)S(1)}, u32[]{:S(2)}, u32[]{:S(2)}) %collective-permute-start.1) | collective-permute-done | bytes 1966112 | tf_op jit(solution)/shard_map/ppermute | solution.py:71
  95.6 1.8 %fusion.1 = (bf16[160,6144]{1,0:T(8,128)(2,1)S(1)}, f32[160]{0:T(256)S(1)}) fusion(bf16[160,6144]{1,0:T(8,128)(2,1)S(1)} %collective-permute-done.1, bf16[160,6144]{1,0:T(8,128)(2,1)S(1)} %convolution_convert_fusion, bf16[160,6144]{1,0:T(8,128)(2,1)S(1)} %get-tuple-element.31, pred[]{:T(512)S(6)} %eq.45, bf16[160,6144]{1,0:T(8,128)(2,1)} %collective-permute-done, ...), kind=kLoop, calls=%fused_computation.6 | loop fusion | flops 8847200 | bytes 11797121 | tf_op jit(solution)/shard_map/convert_element_type | solution.py:73
  97.3 0.2 copy.70
  97.7 1.5 pad_maximum_fusion
  99.2 4.4 %all-to-all-start.2 = ((bf16[16,161,384]{2,1,0:T(8,128)(2,1)}), bf16[16,161,384]{2,1,0:T(8,128)(2,1)}, u32[]{:S(2)}, u32[]{:S(2)}) async-start(bf16[16,161,384]{2,1,0:T(8,128)(2,1)} %pad_maximum_fusion), calls=%async_computation.2 | async-start | bytes 4128768 | tf_op jit(solution)/shard_map/all_to_all | solution.py:82
  103.7 27.7 %all-to-all-done.2 = bf16[16,161,384]{2,1,0:T(8,128)(2,1)} async-done(((bf16[16,161,384]{2,1,0:T(8,128)(2,1)}), bf16[16,161,384]{2,1,0:T(8,128)(2,1)}, u32[]{:S(2)}, u32[]{:S(2)}) %all-to-all-start.2) | async-done | bytes 1978400 | tf_op jit(solution)/shard_map/all_to_all | solution.py:82
  131.3 1.8 %convert_element_type.111 = f32[16,161,384]{2,1,0:T(8,128)S(1)} convert(bf16[16,161,384]{2,1,0:T(8,128)(2,1)} %all-to-all-done.2) | non-fusion elementwise | flops 989184 | bytes 5935104 | tf_op jit(solution)/shard_map/convert_element_type | solution.py:82
  133.8 0.8 pad_maximum_fusion.2
  134.6 7.1 %all-to-all-start.3 = ((bf16[32,6,384]{2,1,0:T(8,128)(2,1)}), bf16[32,6,384]{2,1,0:T(8,128)(2,1)S(1)}, u32[]{:S(2)}, u32[]{:S(2)}) async-start(bf16[32,6,384]{2,1,0:T(8,128)(2,1)} %pad_maximum_fusion.2), calls=%async_computation.3 | async-start | bytes 393216 | tf_op jit(solution)/shard_map/all_to_all | solution.py:96
  141.8 18.8 %all-to-all-done.3 = bf16[32,6,384]{2,1,0:T(8,128)(2,1)S(1)} async-done(((bf16[32,6,384]{2,1,0:T(8,128)(2,1)}), bf16[32,6,384]{2,1,0:T(8,128)(2,1)S(1)}, u32[]{:S(2)}, u32[]{:S(2)}) %all-to-all-start.3) | async-done | bytes 147488 | tf_op jit(solution)/shard_map/all_to_all | solution.py:96
  160.8 0.2 fusion.22
  161.4 0.8 multiply_reduce_fusion.1
  162.2 0.6 copy.63
  162.8 0.7 reduce_sum.110
  (47 shorter events, 2.3 us)
Async XLA Ops:
  0.6 83.0 %copy-start = (bf16[1,6144,128]{2,1,0:T(8,128)(2,1)S(1)}, bf16[1,6144,128]{2,1,0:T(8,128)(2,1)}, u32[]{:S(2)}) copy-start(bf16[1,6144,128]{2,1,0:T(8,128)(2,1)} %param.11) | copy-start | bytes 4718596
  72.3 8.5 %collective-permute-start = (bf16[160,6144]{1,0:T(8,128)(2,1)S(1)}, bf16[160,6144]{1,0:T(8,128)(2,1)}, u32[]{:S(2)}, u32[]{:S(2)}) collective-permute-start(bf16[160,6144]{1,0:T(8,128)(2,1)S(1)} %bitcast.41), channel_id=1, source_target_pairs={{0,4},{4,0},{8,12},{12,8},{16,20},{20,16},{24,28},{28,24},{32,36},... | collective-permute-start | bytes 5898248 | tf_op jit(solution)/shard_map/ppermute | solution.py:45
  83.6 2.5 %copy-start.1 = (bf16[1,128,6144]{2,1,0:T(8,128)(2,1)S(1)}, bf16[1,128,6144]{2,1,0:T(8,128)(2,1)}, u32[]{:S(2)}) copy-start(bf16[1,128,6144]{2,1,0:T(8,128)(2,1)} %param.12) | copy-start | bytes 4718596
  86.8 1.4 copy-start.2
  89.7 5.9 %collective-permute-start.1 = (bf16[160,6144]{1,0:T(8,128)(2,1)S(1)}, bf16[160,6144]{1,0:T(8,128)(2,1)S(1)}, u32[]{:S(2)}, u32[]{:S(2)}) collective-permute-start(bf16[160,6144]{1,0:T(8,128)(2,1)S(1)} %get-tuple-element.30), channel_id=1, source_target_pairs={{0,4},{4,0},{8,12},{12,8},{16,20},{20,16},{24,28},{28,24},{32,36},... | collective-permute-start | bytes 5898248 | tf_op jit(solution)/shard_map/ppermute | solution.py:71
  99.2 32.2 %all-to-all-start.2 = ((bf16[16,161,384]{2,1,0:T(8,128)(2,1)}), bf16[16,161,384]{2,1,0:T(8,128)(2,1)}, u32[]{:S(2)}, u32[]{:S(2)}) async-start(bf16[16,161,384]{2,1,0:T(8,128)(2,1)} %pad_maximum_fusion), calls=%async_computation.2 | async-start | bytes 4128768 | tf_op jit(solution)/shard_map/all_to_all | solution.py:82
  133.2 8.5 %copy-start.3 = (f32[16,2]{0,1:T(2,128)S(1)}, f32[16,2]{0,1:T(2,128)}, u32[]{:S(2)}) copy-start(f32[16,2]{0,1:T(2,128)} %param.9) | copy-start | bytes 388
  134.6 25.9 %all-to-all-start.3 = ((bf16[32,6,384]{2,1,0:T(8,128)(2,1)}), bf16[32,6,384]{2,1,0:T(8,128)(2,1)S(1)}, u32[]{:S(2)}, u32[]{:S(2)}) async-start(bf16[32,6,384]{2,1,0:T(8,128)(2,1)} %pad_maximum_fusion.2), calls=%async_computation.3 | async-start | bytes 393216 | tf_op jit(solution)/shard_map/all_to_all | solution.py:96

commit v7 on v6

--- a/solution.py
+++ b/solution.py
@@ -66,22 +66,22 @@
         d_up_h, up_proj, contract_last, preferred_element_type=jnp.float32
     )
     dx_terms = dx_terms.astype(jnp.bfloat16)
-    keep = jnp.where(first_core, out_terms, dx_terms)
-    give = jnp.where(first_core, dx_terms, out_terms)
-    got = lax.ppermute(give, "expert", partner)
-    both_f32 = keep.astype(jnp.float32) + got.astype(jnp.float32)
-    both = both_f32.astype(jnp.bfloat16)
-    row_dots = jnp.sum(rows_dy.astype(jnp.float32) * both_f32, axis=1)
+    row_dots = jnp.sum(rows_dy.astype(jnp.float32) * out_terms.astype(jnp.float32), axis=1)
     dots_hi = row_dots.astype(jnp.bfloat16)
     dots_lo = (row_dots - dots_hi.astype(jnp.float32)).astype(jnp.bfloat16)
     dots_row = jnp.concatenate(
         [dots_hi, dots_lo, jnp.zeros((feat - 2 * rows_n,), jnp.bfloat16)]
     ).reshape(1, 1, feat)
+    keep = jnp.where(first_core, out_terms, dx_terms)
+    give = jnp.where(first_core, dx_terms, out_terms)
+    got = lax.ppermute(give, "expert", partner)
+    both = (keep.astype(jnp.float32) + got.astype(jnp.float32)).astype(jnp.bfloat16)
     terms = both.reshape(rows_n, planes, feat).transpose(1, 0, 2)
     terms = jnp.concatenate([terms, jnp.broadcast_to(dots_row, (planes, 1, feat))], axis=1)
-    reduced = lax.all_to_all(terms, ("pipe", "tensor"), 0, 0, tiled=True).astype(jnp.float32)
-    shares = jnp.sum(reduced[:, :rows_n], axis=0).astype(jnp.bfloat16)
-    dots_sum = jnp.sum(reduced[:, rows_n, :rows_n] + reduced[:, rows_n, rows_n:2 * rows_n], axis=0)
+    reduced = lax.all_to_all(terms, ("pipe", "tensor"), 0, 0, tiled=True)
+    shares = jnp.sum(reduced[:, :rows_n].astype(jnp.float32), axis=0).astype(jnp.bfloat16)
+    dots_in = reduced[:, rows_n, : 2 * rows_n].astype(jnp.float32)
+    dots_sum = jnp.sum(dots_in[:, :rows_n] + dots_in[:, rows_n:], axis=0)
     back_hi = dots_sum.astype(jnp.bfloat16)
     back_lo = (dots_sum - back_hi.astype(jnp.float32)).astype(jnp.bfloat16)
     back_dots = jnp.concatenate(
@@ -94,11 +94,12 @@
     ).reshape(devices_all, 1, feat)
     back_send = jnp.concatenate([shares.reshape(devices_all, capacity, feat), back_dots], axis=1)
     back = lax.all_to_all(back_send, "expert", split_axis=0, concat_axis=0, tiled=True)
-    back = back.astype(jnp.float32).reshape(experts, group // 2, 2, capacity + 1, feat)
-    back_rows = jnp.sum(back[:, :, :, :capacity], axis=1).astype(jnp.bfloat16)
+    back = back.reshape(experts, group // 2, 2, capacity + 1, feat)
+    back_rows = jnp.sum(back[:, :, :, :capacity].astype(jnp.float32), axis=1).astype(jnp.bfloat16)
     back_rows = back_rows.transpose(0, 2, 1, 3).reshape(slots, 2 * feat)
+    back_dots = back[:, :, :, capacity, : 2 * capacity].astype(jnp.float32)
     slot_dots = jnp.sum(
-        back[:, :, 0, capacity, :capacity] + back[:, :, 0, capacity, capacity:2 * capacity], axis=1
+        back_dots[..., :capacity] + back_dots[..., capacity:], axis=(1, 2)
     ).reshape(slots)
     assign = picks.T.astype(jnp.bfloat16)
     a_both = jnp.dot(assign, back_rows, preferred_element_type=jnp.float32)

time: 164 us -> 165 us (level)
    convert_element_type x2 -> x3, other arithmetic: 3.62 us -> 2.74 us  [the longest x1 1.81 us: per_device(): (keep.astype(jnp.float32) + got.astype(jnp.float32)).astype(jnp.bfloat16)]
where the time goes in v7:
time: 165 us; the launch traced here: 164 us
  blocking collectives  67 us (41%)
  waiting for transfers between devices  54 us (33%)
  starting transfers between devices  18.2 us (11%)
  other arithmetic  10.7 us (6%)
  matrix products  9.29 us (6%)
  local copies, waits for them, and re-layouts  3.97 us (2%)
    all_to_all x1, blocking collectives, per_device(): lax.all_to_all(send, 'expert', split_axis=0, concat_axis=0, tiled=True)  35.2 us
    all_to_all x1, blocking collectives, per_device(): gathered = lax.all_to_all(spread, ('pipe', 'tensor'), 0, 0, tiled=True)  31.8 us
    all_to_all x1, waiting for transfers between devices, per_device(): reduced = lax.all_to_all(terms, ('pipe', 'tensor'), 0, 0, tiled=True)  27.6 us
    all_to_all x1, waiting for transfers between devices, per_device(): lax.all_to_all(back_send, 'expert', split_axis=0, concat_axis=0, tiled=True)  18.8 us
    all_to_all x1, starting transfers between devices, per_device(): lax.all_to_all(back_send, 'expert', split_axis=0, concat_axis=0, tiled=True)  7.08 us
    ppermute x1, starting transfers between devices, per_device(): other_rows = lax.ppermute(own_rows, 'expert', partner)  4.76 us
    all_to_all x1, starting transfers between devices, per_device(): reduced = lax.all_to_all(terms, ('pipe', 'tensor'), 0, 0, tiled=True)  4.42 us
    ppermute x1, waiting for transfers between devices, per_device(): got = lax.ppermute(give, 'expert', partner)  3.94 us
  transfers between devices with their start and end apart: 4, of which 4 were waited for; matrix products, arithmetic and copies ran while one was open for 0% of the time, Pallas kernels for 0%

profile of v7, /device:TPU:1, one launch (start us, length us, event | category | flops | bytes accessed | tf_op | source)
XLA Modules:
  0.0 164.2 jit_solution(10336333675846409780)
XLA Ops:
  0.6 0.9 copy.54
  2.1 0.7 multiply_add_fusion
  2.8 0.8 select_reduce_fusion.1
  3.6 0.9 fusion.15
  4.7 35.2 %all_to_all.20 = bf16[32,5,384]{2,1,0:T(8,128)(2,1)S(1)} all-to-all(bf16[32,5,384]{2,1,0:T(8,128)(2,1)S(1)} %bitcast.51), channel_id=1, replica_groups=mesh['pipe'=4,'expert'=32,'tensor'=4] {'expert'}, dimensions={0} | all-to-all | bytes 245760 | tf_op jit(solution)/shard_map/all_to_all | solution.py:40
  40.1 31.8 %all_to_all.21 = bf16[16,160,384]{2,1,0:T(8,128)(2,1)S(1)} all-to-all(bf16[16,160,384]{2,1,0:T(8,128)(2,1)S(1)} %broadcast_in_dim.11), channel_id=1, replica_groups=mesh['pipe'=4,'expert'=32,'tensor'=4] {'pipe','tensor'}, dimensions={0} | all-to-all | bytes 3932160 | tf_op jit(solution)/shard_map/all_to_all | solution.py:43
  72.0 0.3 copy.68
  72.3 4.8 %collective-permute-start = (bf16[160,6144]{1,0:T(8,128)(2,1)S(1)}, bf16[160,6144]{1,0:T(8,128)(2,1)}, u32[]{:S(2)}, u32[]{:S(2)}) collective-permute-start(bf16[160,6144]{1,0:T(8,128)(2,1)S(1)} %bitcast.41), channel_id=1, source_target_pairs={{0,4},{4,0},{8,12},{12,8},{16,20},{20,16},{24,28},{28,24},{32,36},... | collective-permute-start | bytes 5898248 | tf_op jit(solution)/shard_map/ppermute | solution.py:45
  77.1 3.7 %collective-permute-done = bf16[160,6144]{1,0:T(8,128)(2,1)} collective-permute-done((bf16[160,6144]{1,0:T(8,128)(2,1)S(1)}, bf16[160,6144]{1,0:T(8,128)(2,1)}, u32[]{:S(2)}, u32[]{:S(2)}) %collective-permute-start) | collective-permute-done | bytes 1966112 | tf_op jit(solution)/shard_map/ppermute | solution.py:45
  80.8 2.9 %fusion.9 = f32[160,128]{1,0:T(8,128)S(1)} fusion(bf16[1,6144,128]{2,1,0:T(8,128)(2,1)} %param.10, bf16[160,6144]{1,0:T(8,128)(2,1)S(1)} %bitcast.42, bf16[160,6144]{1,0:T(8,128)(2,1)} %collective-permute-done, pred[]{:T(512)S(6)} %eq.45), kind=kOutput, calls=%fused_computation.19 | convolution fusion | flops 252641280 | bytes 5586945 | tf_op jit(solution)/shard_map/dot_general | solution.py:52
  83.6 2.5 %fusion.5 = f32[160,128]{1,0:T(8,128)S(1)} fusion(bf16[1,6144,128]{2,1,0:T(8,128)(2,1)S(1)} %copy-done, bf16[160,6144]{1,0:T(8,128)(2,1)S(1)} %bitcast.43, bf16[160,6144]{1,0:T(8,128)(2,1)} %collective-permute-done, pred[]{:T(512)S(6)} %eq.45), kind=kOutput, calls=%fused_computation.15 | convolution fusion | flops 252641280 | bytes 5586945 | tf_op jit(solution)/shard_map/dot_general | solution.py:53
  86.2 0.7 convolution_convert_fusion
  86.9 0.7 fusion.1
  87.6 0.7 copy-done.2
  88.3 0.7 fusion.7
  88.9 0.8 broadcast_select_fusion
  89.7 1.9 %collective-permute-start.1 = (bf16[160,6144]{1,0:T(8,128)(2,1)S(1)}, bf16[160,6144]{1,0:T(8,128)(2,1)S(1)}, u32[]{:S(2)}, u32[]{:S(2)}) collective-permute-start(bf16[160,6144]{1,0:T(8,128)(2,1)S(1)} %get-tuple-element.30), channel_id=1, source_target_pairs={{0,4},{4,0},{8,12},{12,8},{16,20},{20,16},{24,28},{28,24},{32,36},... | collective-permute-start | bytes 5898248 | tf_op jit(solution)/shard_map/ppermute | solution.py:77
  91.6 3.9 %collective-permute-done.1 = bf16[160,6144]{1,0:T(8,128)(2,1)S(1)} collective-permute-done((bf16[160,6144]{1,0:T(8,128)(2,1)S(1)}, bf16[160,6144]{1,0:T(8,128)(2,1)S(1)}, u32[]{:S(2)}, u32[]{:S(2)}) %collective-permute-start.1) | collective-permute-done | bytes 1966112 | tf_op jit(solution)/shard_map/ppermute | solution.py:77
  95.6 1.8 %add_convert_fusion = (bf16[160,6144]{1,0:T(8,128)(2,1)S(1)}, f32[160]{0:T(256)S(1)}) fusion(bf16[160,6144]{1,0:T(8,128)(2,1)S(1)} %collective-permute-done.1, bf16[160,6144]{1,0:T(8,128)(2,1)S(1)} %convolution_convert_fusion, bf16[160,6144]{1,0:T(8,128)(2,1)S(1)} %get-tuple-element.31, pred[]{:T(512)S(6)} %eq.45, bf16[160,6144]{1,0:T(8,128)(2,1)} %collective-permute-done, ...), kind=kLoop, calls=%fused_computation.4 | loop fusion | flops 9830240 | bytes 11797121 | tf_op jit(solution)/shard_map/convert_element_type | solution.py:78
  97.4 0.2 copy.72
  97.7 1.5 pad_maximum_fusion
  99.2 4.4 %all-to-all-start.2 = ((bf16[16,161,384]{2,1,0:T(8,128)(2,1)}), bf16[16,161,384]{2,1,0:T(8,128)(2,1)}, u32[]{:S(2)}, u32[]{:S(2)}) async-start(bf16[16,161,384]{2,1,0:T(8,128)(2,1)} %pad_maximum_fusion), calls=%async_computation.2 | async-start | bytes 4128768 | tf_op jit(solution)/shard_map/all_to_all | solution.py:81
  103.7 27.6 %all-to-all-done.2 = bf16[16,161,384]{2,1,0:T(8,128)(2,1)} async-done(((bf16[16,161,384]{2,1,0:T(8,128)(2,1)}), bf16[16,161,384]{2,1,0:T(8,128)(2,1)}, u32[]{:S(2)}, u32[]{:S(2)}) %all-to-all-start.2) | async-done | bytes 1978400 | tf_op jit(solution)/shard_map/all_to_all | solution.py:81
  131.4 1.8 %slice_reduce_fusion = bf16[160,384]{1,0:T(8,128)(2,1)S(1)} fusion(bf16[16,161,384]{2,1,0:T(8,128)(2,1)} %all-to-all-done.2), kind=kLoop, calls=%fused_computation.7 | loop fusion | flops 921600 | bytes 2088960 | tf_op jit(solution)/shard_map/reduce_sum | solution.py:82
  133.3 0.9 slice_convert_fusion.1
  134.5 0.8 pad_maximum_fusion.2
  135.3 7.1 %all-to-all-start.3 = ((bf16[32,6,384]{2,1,0:T(8,128)(2,1)}), bf16[32,6,384]{2,1,0:T(8,128)(2,1)S(1)}, u32[]{:S(2)}, u32[]{:S(2)}) async-start(bf16[32,6,384]{2,1,0:T(8,128)(2,1)} %pad_maximum_fusion.2), calls=%async_computation.3 | async-start | bytes 393216 | tf_op jit(solution)/shard_map/all_to_all | solution.py:96
  142.5 18.8 %all-to-all-done.3 = bf16[32,6,384]{2,1,0:T(8,128)(2,1)S(1)} async-done(((bf16[32,6,384]{2,1,0:T(8,128)(2,1)}), bf16[32,6,384]{2,1,0:T(8,128)(2,1)S(1)}, u32[]{:S(2)}, u32[]{:S(2)}) %all-to-all-start.3) | async-done | bytes 147488 | tf_op jit(solution)/shard_map/all_to_all | solution.py:96
  161.4 0.2 fusion.22
  162.1 0.8 multiply_reduce_fusion.1
  162.9 0.6 copy.63
  163.5 0.7 reduce_sum.116
  (48 shorter events, 2.3 us)
Async XLA Ops:
  0.6 83.0 %copy-start = (bf16[1,6144,128]{2,1,0:T(8,128)(2,1)S(1)}, bf16[1,6144,128]{2,1,0:T(8,128)(2,1)}, u32[]{:S(2)}) copy-start(bf16[1,6144,128]{2,1,0:T(8,128)(2,1)} %param.11) | copy-start | bytes 4718596
  72.3 8.5 %collective-permute-start = (bf16[160,6144]{1,0:T(8,128)(2,1)S(1)}, bf16[160,6144]{1,0:T(8,128)(2,1)}, u32[]{:S(2)}, u32[]{:S(2)}) collective-permute-start(bf16[160,6144]{1,0:T(8,128)(2,1)S(1)} %bitcast.41), channel_id=1, source_target_pairs={{0,4},{4,0},{8,12},{12,8},{16,20},{20,16},{24,28},{28,24},{32,36},... | collective-permute-start | bytes 5898248 | tf_op jit(solution)/shard_map/ppermute | solution.py:45
  83.6 2.5 %copy-start.1 = (bf16[1,128,6144]{2,1,0:T(8,128)(2,1)S(1)}, bf16[1,128,6144]{2,1,0:T(8,128)(2,1)}, u32[]{:S(2)}) copy-start(bf16[1,128,6144]{2,1,0:T(8,128)(2,1)} %param.12) | copy-start | bytes 4718596
  86.8 1.4 copy-start.2
  89.7 5.9 %collective-permute-start.1 = (bf16[160,6144]{1,0:T(8,128)(2,1)S(1)}, bf16[160,6144]{1,0:T(8,128)(2,1)S(1)}, u32[]{:S(2)}, u32[]{:S(2)}) collective-permute-start(bf16[160,6144]{1,0:T(8,128)(2,1)S(1)} %get-tuple-element.30), channel_id=1, source_target_pairs={{0,4},{4,0},{8,12},{12,8},{16,20},{20,16},{24,28},{28,24},{32,36},... | collective-permute-start | bytes 5898248 | tf_op jit(solution)/shard_map/ppermute | solution.py:77
  99.2 32.2 %all-to-all-start.2 = ((bf16[16,161,384]{2,1,0:T(8,128)(2,1)}), bf16[16,161,384]{2,1,0:T(8,128)(2,1)}, u32[]{:S(2)}, u32[]{:S(2)}) async-start(bf16[16,161,384]{2,1,0:T(8,128)(2,1)} %pad_maximum_fusion), calls=%async_computation.2 | async-start | bytes 4128768 | tf_op jit(solution)/shard_map/all_to_all | solution.py:81
  103.6 38.7 %copy-start.3 = (f32[16,2]{0,1:T(2,128)S(1)}, f32[16,2]{0,1:T(2,128)}, u32[]{:S(2)}) copy-start(f32[16,2]{0,1:T(2,128)} %param.9) | copy-start | bytes 388
  135.3 25.9 %all-to-all-start.3 = ((bf16[32,6,384]{2,1,0:T(8,128)(2,1)}), bf16[32,6,384]{2,1,0:T(8,128)(2,1)S(1)}, u32[]{:S(2)}, u32[]{:S(2)}) async-start(bf16[32,6,384]{2,1,0:T(8,128)(2,1)} %pad_maximum_fusion.2), calls=%async_computation.3 | async-start | bytes 393216 | tf_op jit(solution)/shard_map/all_to_all | solution.py:96

commit v8 on v7

--- a/solution.py
+++ b/solution.py
@@ -66,7 +66,7 @@
         d_up_h, up_proj, contract_last, preferred_element_type=jnp.float32
     )
     dx_terms = dx_terms.astype(jnp.bfloat16)
-    row_dots = jnp.sum(rows_dy.astype(jnp.float32) * out_terms.astype(jnp.float32), axis=1)
+    row_dots = jnp.sum(hidden.astype(jnp.float32) * d_hidden, axis=1)
     dots_hi = row_dots.astype(jnp.bfloat16)
     dots_lo = (row_dots - dots_hi.astype(jnp.float32)).astype(jnp.bfloat16)
     dots_row = jnp.concatenate(
@@ -75,9 +75,11 @@
     keep = jnp.where(first_core, out_terms, dx_terms)
     give = jnp.where(first_core, dx_terms, out_terms)
     got = lax.ppermute(give, "expert", partner)
+    dots_line = jnp.broadcast_to(dots_row.reshape(1, feat), (planes, feat)).reshape(1, planes * feat)
+    keep = jnp.concatenate([keep, dots_line], axis=0)
+    got = jnp.concatenate([got, jnp.zeros((1, planes * feat), jnp.bfloat16)], axis=0)
     both = (keep.astype(jnp.float32) + got.astype(jnp.float32)).astype(jnp.bfloat16)
-    terms = both.reshape(rows_n, planes, feat).transpose(1, 0, 2)
-    terms = jnp.concatenate([terms, jnp.broadcast_to(dots_row, (planes, 1, feat))], axis=1)
+    terms = both.reshape(rows_n + 1, planes, feat).transpose(1, 0, 2)
     reduced = lax.all_to_all(terms, ("pipe", "tensor"), 0, 0, tiled=True)
     shares = jnp.sum(reduced[:, :rows_n].astype(jnp.float32), axis=0).astype(jnp.bfloat16)
     dots_in = reduced[:, rows_n, : 2 * rows_n].astype(jnp.float32)

time: 165 us -> 167 us (1.012)
  waiting for transfers between devices: 54 us -> 59.3 us
  other arithmetic: 10.7 us -> 8.06 us
  starting transfers between devices: 18.2 us -> 15.6 us
  local copies, waits for them, and re-layouts: 3.97 us -> 6.05 us
    all_to_all x1, waiting for transfers between devices: 27.6 us -> 33.1 us  [per_device(): reduced = lax.all_to_all(terms, ('pipe', 'tensor'), 0, 0, tiled=True)]
    all_to_all x1, starting transfers between devices: 7.08 us -> 4.47 us  [per_device(): lax.all_to_all(back_send, 'expert', split_axis=0, concat_axis=0, tiled=True)]
    reshape x1 -> x2, local copies, waits for them, and re-layouts: 0.2 us -> 1.93 us  [per_device(): terms = both.reshape(rows_n + 1, planes, feat).transpose(1, 0, 2)]
where the time goes in v8:
time: 167 us; the launch traced here: 166 us
  blocking collectives  67 us (40%)
  waiting for transfers between devices  59.3 us (36%)
  starting transfers between devices  15.6 us (9%)
  matrix products  9.3 us (6%)
  other arithmetic  8.06 us (5%)
  local copies, waits for them, and re-layouts  6.05 us (4%)
    all_to_all x1, blocking collectives, per_device(): lax.all_to_all(send, 'expert', split_axis=0, concat_axis=0, tiled=True)  35.2 us
    all_to_all x1, waiting for transfers between devices, per_device(): reduced = lax.all_to_all(terms, ('pipe', 'tensor'), 0, 0, tiled=True)  33.1 us
    all_to_all x1, blocking collectives, per_device(): gathered = lax.all_to_all(spread, ('pipe', 'tensor'), 0, 0, tiled=True)  31.8 us
    all_to_all x1, waiting for transfers between devices, per_device(): lax.all_to_all(back_send, 'expert', split_axis=0, concat_axis=0, tiled=True)  18.8 us
    ppermute x1, starting transfers between devices, per_device(): other_rows = lax.ppermute(own_rows, 'expert', partner)  4.76 us
    all_to_all x1, starting transfers between devices, per_device(): lax.all_to_all(back_send, 'expert', split_axis=0, concat_axis=0, tiled=True)  4.47 us
    all_to_all x1, starting transfers between devices, per_device(): reduced = lax.all_to_all(terms, ('pipe', 'tensor'), 0, 0, tiled=True)  4.42 us
    ppermute x1, waiting for transfers between devices, per_device(): got = lax.ppermute(give, 'expert', partner)  3.8 us
  transfers between devices with their start and end apart: 4, of which 4 were waited for; matrix products, arithmetic and copies ran while one was open for 0% of the time, Pallas kernels for 0%

profile of v8, /device:TPU:1, one launch (start us, length us, event | category | flops | bytes accessed | tf_op | source)
XLA Modules:
  0.0 166.3 jit_solution(35304006316098111)
XLA Ops:
  0.6 0.9 copy.54
  2.1 0.7 multiply_add_fusion
  2.8 0.8 select_reduce_fusion.1
  3.6 0.9 fusion.16
  4.7 35.2 %all_to_all.20 = bf16[32,5,384]{2,1,0:T(8,128)(2,1)S(1)} all-to-all(bf16[32,5,384]{2,1,0:T(8,128)(2,1)S(1)} %bitcast.57), channel_id=1, replica_groups=mesh['pipe'=4,'expert'=32,'tensor'=4] {'expert'}, dimensions={0} | all-to-all | bytes 245760 | tf_op jit(solution)/shard_map/all_to_all | solution.py:40
  40.1 31.8 %all_to_all.21 = bf16[16,160,384]{2,1,0:T(8,128)(2,1)S(1)} all-to-all(bf16[16,160,384]{2,1,0:T(8,128)(2,1)S(1)} %broadcast_in_dim.11), channel_id=1, replica_groups=mesh['pipe'=4,'expert'=32,'tensor'=4] {'pipe','tensor'}, dimensions={0} | all-to-all | bytes 3932160 | tf_op jit(solution)/shard_map/all_to_all | solution.py:43
  72.0 0.3 copy.67
  72.3 4.8 %collective-permute-start = (bf16[160,6144]{1,0:T(8,128)(2,1)S(1)}, bf16[160,6144]{1,0:T(8,128)(2,1)}, u32[]{:S(2)}, u32[]{:S(2)}) collective-permute-start(bf16[160,6144]{1,0:T(8,128)(2,1)S(1)} %bitcast.51), channel_id=1, source_target_pairs={{0,4},{4,0},{8,12},{12,8},{16,20},{20,16},{24,28},{28,24},{32,36},... | collective-permute-start | bytes 5898248 | tf_op jit(solution)/shard_map/ppermute | solution.py:45
  77.1 3.7 %collective-permute-done = bf16[160,6144]{1,0:T(8,128)(2,1)} collective-permute-done((bf16[160,6144]{1,0:T(8,128)(2,1)S(1)}, bf16[160,6144]{1,0:T(8,128)(2,1)}, u32[]{:S(2)}, u32[]{:S(2)}) %collective-permute-start) | collective-permute-done | bytes 1966112 | tf_op jit(solution)/shard_map/ppermute | solution.py:45
  80.8 2.9 %fusion.11 = f32[160,128]{1,0:T(8,128)S(1)} fusion(bf16[1,6144,128]{2,1,0:T(8,128)(2,1)} %param.10, bf16[160,6144]{1,0:T(8,128)(2,1)S(1)} %bitcast.52, bf16[160,6144]{1,0:T(8,128)(2,1)} %collective-permute-done, pred[]{:T(512)S(6)} %eq.45), kind=kOutput, calls=%fused_computation.19 | convolution fusion | flops 252641280 | bytes 5586945 | tf_op jit(solution)/shard_map/dot_general | solution.py:52
  83.6 2.5 %fusion.7 = f32[160,128]{1,0:T(8,128)S(1)} fusion(bf16[1,6144,128]{2,1,0:T(8,128)(2,1)S(1)} %copy-done, bf16[160,6144]{1,0:T(8,128)(2,1)S(1)} %bitcast.53, bf16[160,6144]{1,0:T(8,128)(2,1)} %collective-permute-done, pred[]{:T(512)S(6)} %eq.45), kind=kOutput, calls=%fused_computation.15 | convolution fusion | flops 252641280 | bytes 5586945 | tf_op jit(solution)/shard_map/dot_general | solution.py:53
  86.2 0.8 multiply_reduce_fusion
  87.0 0.6 copy-done.2
  87.6 0.7 fusion.9
  88.3 0.7 convolution_convert_fusion
  88.9 0.7 broadcast_select_fusion
  89.6 1.9 %collective-permute-start.1 = (bf16[160,6144]{1,0:T(8,128)(2,1)S(1)}, bf16[160,6144]{1,0:T(8,128)(2,1)S(1)}, u32[]{:S(2)}, u32[]{:S(2)}) collective-permute-start(bf16[160,6144]{1,0:T(8,128)(2,1)S(1)} %get-tuple-element.26), channel_id=1, source_target_pairs={{0,4},{4,0},{8,12},{12,8},{16,20},{20,16},{24,28},{28,24},{32,36},... | collective-permute-start | bytes 5898248 | tf_op jit(solution)/shard_map/ppermute | solution.py:77
  91.7 3.8 %collective-permute-done.1 = bf16[160,6144]{1,0:T(8,128)(2,1)S(1)} collective-permute-done((bf16[160,6144]{1,0:T(8,128)(2,1)S(1)}, bf16[160,6144]{1,0:T(8,128)(2,1)S(1)}, u32[]{:S(2)}, u32[]{:S(2)}) %collective-permute-start.1) | collective-permute-done | bytes 1966112 | tf_op jit(solution)/shard_map/ppermute | solution.py:77
  95.5 0.6 add_convert_fusion
  96.1 0.4 copy.69
  96.6 0.2 slice.61
  96.8 1.7 %copy.73 = bf16[161,16,384]{2,0,1:T(8,128)(2,1)} copy(bf16[161,16,384]{2,1,0:T(8,128)(2,1)S(1)} %slice.61) | data formatting | bytes 3956736 | tf_op jit(solution)/shard_map/reshape | solution.py:82
  98.5 4.4 %all-to-all-start.2 = ((bf16[16,161,384]{2,1,0:T(8,128)(2,1)}), bf16[16,161,384]{2,1,0:T(8,128)(2,1)}, u32[]{:S(2)}, u32[]{:S(2)}) async-start(bf16[16,161,384]{2,1,0:T(8,128)(2,1)} %bitcast.47), calls=%async_computation.2 | async-start | bytes 4128768 | tf_op jit(solution)/shard_map/all_to_all | solution.py:83
  103.0 33.1 %all-to-all-done.2 = bf16[16,161,384]{2,1,0:T(8,128)(2,1)} async-done(((bf16[16,161,384]{2,1,0:T(8,128)(2,1)}), bf16[16,161,384]{2,1,0:T(8,128)(2,1)}, u32[]{:S(2)}, u32[]{:S(2)}) %all-to-all-start.2) | async-done | bytes 1978400 | tf_op jit(solution)/shard_map/all_to_all | solution.py:83
  136.1 1.8 %slice_reduce_fusion = bf16[160,384]{1,0:T(8,128)(2,1)S(1)} fusion(bf16[16,161,384]{2,1,0:T(8,128)(2,1)} %all-to-all-done.2), kind=kLoop, calls=%fused_computation.5 | loop fusion | flops 921600 | bytes 2088960 | tf_op jit(solution)/shard_map/reduce_sum | solution.py:84
  138.0 0.9 slice_convert_fusion.1
  139.2 0.8 pad_maximum_fusion.1
  140.0 4.5 %all-to-all-start.3 = ((bf16[32,6,384]{2,1,0:T(8,128)(2,1)}), bf16[32,6,384]{2,1,0:T(8,128)(2,1)S(1)}, u32[]{:S(2)}, u32[]{:S(2)}) async-start(bf16[32,6,384]{2,1,0:T(8,128)(2,1)} %pad_maximum_fusion.1), calls=%async_computation.3 | async-start | bytes 393216 | tf_op jit(solution)/shard_map/all_to_all | solution.py:98
  144.6 18.8 %all-to-all-done.3 = bf16[32,6,384]{2,1,0:T(8,128)(2,1)S(1)} async-done(((bf16[32,6,384]{2,1,0:T(8,128)(2,1)}), bf16[32,6,384]{2,1,0:T(8,128)(2,1)S(1)}, u32[]{:S(2)}, u32[]{:S(2)}) %all-to-all-start.3) | async-done | bytes 147488 | tf_op jit(solution)/shard_map/all_to_all | solution.py:98
  164.2 0.8 multiply_reduce_fusion.1
  165.0 0.6 copy.63
  165.6 0.7 reduce_sum.116
  (50 shorter events, 2.5 us)
Async XLA Ops:
  0.6 83.0 %copy-start = (bf16[1,6144,128]{2,1,0:T(8,128)(2,1)S(1)}, bf16[1,6144,128]{2,1,0:T(8,128)(2,1)}, u32[]{:S(2)}) copy-start(bf16[1,6144,128]{2,1,0:T(8,128)(2,1)} %param.11) | copy-start | bytes 4718596
  72.3 8.5 %collective-permute-start = (bf16[160,6144]{1,0:T(8,128)(2,1)S(1)}, bf16[160,6144]{1,0:T(8,128)(2,1)}, u32[]{:S(2)}, u32[]{:S(2)}) collective-permute-start(bf16[160,6144]{1,0:T(8,128)(2,1)S(1)} %bitcast.51), channel_id=1, source_target_pairs={{0,4},{4,0},{8,12},{12,8},{16,20},{20,16},{24,28},{28,24},{32,36},... | collective-permute-start | bytes 5898248 | tf_op jit(solution)/shard_map/ppermute | solution.py:45
  83.6 2.5 %copy-start.1 = (bf16[1,128,6144]{2,1,0:T(8,128)(2,1)S(1)}, bf16[1,128,6144]{2,1,0:T(8,128)(2,1)}, u32[]{:S(2)}) copy-start(bf16[1,128,6144]{2,1,0:T(8,128)(2,1)} %param.12) | copy-start | bytes 4718596
  86.2 1.4 copy-start.2
  89.6 5.9 %collective-permute-start.1 = (bf16[160,6144]{1,0:T(8,128)(2,1)S(1)}, bf16[160,6144]{1,0:T(8,128)(2,1)S(1)}, u32[]{:S(2)}, u32[]{:S(2)}) collective-permute-start(bf16[160,6144]{1,0:T(8,128)(2,1)S(1)} %get-tuple-element.26), channel_id=1, source_target_pairs={{0,4},{4,0},{8,12},{12,8},{16,20},{20,16},{24,28},{28,24},{32,36},... | collective-permute-start | bytes 5898248 | tf_op jit(solution)/shard_map/ppermute | solution.py:77
  98.5 37.6 %all-to-all-start.2 = ((bf16[16,161,384]{2,1,0:T(8,128)(2,1)}), bf16[16,161,384]{2,1,0:T(8,128)(2,1)}, u32[]{:S(2)}, u32[]{:S(2)}) async-start(bf16[16,161,384]{2,1,0:T(8,128)(2,1)} %bitcast.47), calls=%async_computation.2 | async-start | bytes 4128768 | tf_op jit(solution)/shard_map/all_to_all | solution.py:83
  102.9 41.6 %copy-start.3 = (f32[16,2]{0,1:T(2,128)S(1)}, f32[16,2]{0,1:T(2,128)}, u32[]{:S(2)}) copy-start(f32[16,2]{0,1:T(2,128)} %param.9) | copy-start | bytes 388
  140.0 23.3 %all-to-all-start.3 = ((bf16[32,6,384]{2,1,0:T(8,128)(2,1)}), bf16[32,6,384]{2,1,0:T(8,128)(2,1)S(1)}, u32[]{:S(2)}, u32[]{:S(2)}) async-start(bf16[32,6,384]{2,1,0:T(8,128)(2,1)} %pad_maximum_fusion.1), calls=%async_computation.3 | async-start | bytes 393216 | tf_op jit(solution)/shard_map/all_to_all | solution.py:98

commit v9 on v6

--- a/solution.py
+++ b/solution.py
@@ -45,6 +45,7 @@
     other_rows = lax.ppermute(own_rows, "expert", partner)
     rows_x = jnp.where(first_core, own_rows, other_rows)
     rows_dy = jnp.where(first_core, other_rows, own_rows)
+    rows_x, rows_dy = lax.optimization_barrier((rows_x, rows_dy))
     gate_proj = w_gate[0]
     up_proj = w_up[0]
     down_proj = w_down[0]

time: 164 us -> 164 us (level)
  waiting for transfers between devices: 54 us -> 58.6 us
  matrix products: 9.29 us -> 5.25 us
  starting transfers between devices: 18.2 us -> 16.2 us
    all_to_all x1, waiting for transfers between devices: 27.7 us -> 32.6 us  [per_device(): lax.all_to_all(terms, ('pipe', 'tensor'), 0, 0, tiled=True)]
    all_to_all x1, starting transfers between devices: 7.08 us -> 4.72 us  [per_device(): lax.all_to_all(back_send, 'expert', split_axis=0, concat_axis=0, tiled=True)]
    dot_general x1, matrix products: 2.85 us -> 0.69 us  [per_device(): h_gate = jnp.dot(rows_x, gate_proj, preferred_element_type=jnp.float32)]
    dot_general x1, matrix products: 2.52 us -> 0.7 us  [per_device(): h_up = jnp.dot(rows_x, up_proj, preferred_element_type=jnp.float32)]
    select_n x0 -> x1, other arithmetic: none -> 1.8 us  [per_device(): rows_dy = jnp.where(first_core, other_rows, own_rows)]
where the time goes in v9:
time: 164 us; the launch traced here: 163 us
  blocking collectives  67 us (41%)
  waiting for transfers between devices  58.6 us (36%)
  starting transfers between devices  16.2 us (10%)
  other arithmetic  11.3 us (7%)
  matrix products  5.25 us (3%)
  local copies, waits for them, and re-layouts  3.97 us (2%)
    all_to_all x1, blocking collectives, per_device(): lax.all_to_all(send, 'expert', split_axis=0, concat_axis=0, tiled=True)  35.2 us
    all_to_all x1, waiting for transfers between devices, per_device(): lax.all_to_all(terms, ('pipe', 'tensor'), 0, 0, tiled=True)  32.6 us
    all_to_all x1, blocking collectives, per_device(): gathered = lax.all_to_all(spread, ('pipe', 'tensor'), 0, 0, tiled=True)  31.8 us
    all_to_all x1, waiting for transfers between devices, per_device(): lax.all_to_all(back_send, 'expert', split_axis=0, concat_axis=0, tiled=True)  18.8 us
    ppermute x1, starting transfers between devices, per_device(): other_rows = lax.ppermute(own_rows, 'expert', partner)  4.76 us
    all_to_all x1, starting transfers between devices, per_device(): lax.all_to_all(back_send, 'expert', split_axis=0, concat_axis=0, tiled=True)  4.72 us
    all_to_all x1, starting transfers between devices, per_device(): lax.all_to_all(terms, ('pipe', 'tensor'), 0, 0, tiled=True)  4.42 us
    ppermute x1, waiting for transfers between devices, per_device(): other_rows = lax.ppermute(own_rows, 'expert', partner)  3.68 us
  transfers between devices with their start and end apart: 4, of which 4 were waited for; matrix products, arithmetic and copies ran while one was open for 0% of the time, Pallas kernels for 0%

profile of v9, /device:TPU:1, one launch (start us, length us, event | category | flops | bytes accessed | tf_op | source)
XLA Modules:
  0.0 163.3 jit_solution(5941831601310447325)
XLA Ops:
  0.6 0.9 copy.54
  2.1 0.7 multiply_add_fusion
  2.8 0.8 select_reduce_fusion.1
  3.6 0.9 fusion.16
  4.7 35.2 %all_to_all.20 = bf16[32,5,384]{2,1,0:T(8,128)(2,1)S(1)} all-to-all(bf16[32,5,384]{2,1,0:T(8,128)(2,1)S(1)} %bitcast.49), channel_id=1, replica_groups=mesh['pipe'=4,'expert'=32,'tensor'=4] {'expert'}, dimensions={0} | all-to-all | bytes 245760 | tf_op jit(solution)/shard_map/all_to_all | solution.py:40
  40.1 31.8 %all_to_all.21 = bf16[16,160,384]{2,1,0:T(8,128)(2,1)S(1)} all-to-all(bf16[16,160,384]{2,1,0:T(8,128)(2,1)S(1)} %broadcast_in_dim.11), channel_id=1, replica_groups=mesh['pipe'=4,'expert'=32,'tensor'=4] {'pipe','tensor'}, dimensions={0} | all-to-all | bytes 3932160 | tf_op jit(solution)/shard_map/all_to_all | solution.py:43
  72.0 0.3 copy.67
  72.3 4.8 %collective-permute-start = (bf16[160,6144]{1,0:T(8,128)(2,1)S(1)}, bf16[160,6144]{1,0:T(8,128)(2,1)}, u32[]{:S(2)}, u32[]{:S(2)}) collective-permute-start(bf16[160,6144]{1,0:T(8,128)(2,1)S(1)} %bitcast.47), channel_id=1, source_target_pairs={{0,4},{4,0},{8,12},{12,8},{16,20},{20,16},{24,28},{28,24},{32,36},... | collective-permute-start | bytes 5898248 | tf_op jit(solution)/shard_map/ppermute | solution.py:45
  77.1 3.7 %collective-permute-done = bf16[160,6144]{1,0:T(8,128)(2,1)} collective-permute-done((bf16[160,6144]{1,0:T(8,128)(2,1)S(1)}, bf16[160,6144]{1,0:T(8,128)(2,1)}, u32[]{:S(2)}, u32[]{:S(2)}) %collective-permute-start) | collective-permute-done | bytes 1966112 | tf_op jit(solution)/shard_map/ppermute | solution.py:45
  80.8 1.8 %broadcast_select_fusion.2 = (bf16[160,6144]{1,0:T(8,128)(2,1)S(1)}, bf16[160,6144]{1,0:T(8,128)(2,1)S(1)}) fusion(bf16[160,6144]{1,0:T(8,128)(2,1)} %collective-permute-done, bf16[160,6144]{1,0:T(8,128)(2,1)S(1)} %bitcast.48, pred[]{:T(512)S(6)} %eq.45), kind=kLoop, calls=%fused_computation.11 | loop fusion | flops 1966080 | bytes 7864321 | tf_op jit(solution)/shard_map/jit(_where)/select_n | solution.py:47
  82.6 0.7 fusion.10
  83.3 0.7 fusion.6
  84.0 0.7 copy-done.1
  84.7 0.7 fusion.2
  85.4 0.7 convolution_convert_fusion
  86.0 0.7 fusion.8
  86.7 0.7 broadcast_select_fusion
  87.5 2.3 %collective-permute-start.1 = (bf16[160,6144]{1,0:T(8,128)(2,1)S(1)}, bf16[160,6144]{1,0:T(8,128)(2,1)S(1)}, u32[]{:S(2)}, u32[]{:S(2)}) collective-permute-start(bf16[160,6144]{1,0:T(8,128)(2,1)S(1)} %get-tuple-element.36), channel_id=1, source_target_pairs={{0,4},{4,0},{8,12},{12,8},{16,20},{20,16},{24,28},{28,24},{32,36},... | collective-permute-start | bytes 5898248 | tf_op jit(solution)/shard_map/ppermute | solution.py:72
  89.8 3.6 %collective-permute-done.1 = bf16[160,6144]{1,0:T(8,128)(2,1)S(1)} collective-permute-done((bf16[160,6144]{1,0:T(8,128)(2,1)S(1)}, bf16[160,6144]{1,0:T(8,128)(2,1)S(1)}, u32[]{:S(2)}, u32[]{:S(2)}) %collective-permute-start.1) | collective-permute-done | bytes 1966112 | tf_op jit(solution)/shard_map/ppermute | solution.py:72
  93.3 1.3 fusion.1
  94.6 0.2 copy.70
  95.0 1.5 pad_maximum_fusion
  96.5 4.4 %all-to-all-start.2 = ((bf16[16,161,384]{2,1,0:T(8,128)(2,1)}), bf16[16,161,384]{2,1,0:T(8,128)(2,1)}, u32[]{:S(2)}, u32[]{:S(2)}) async-start(bf16[16,161,384]{2,1,0:T(8,128)(2,1)} %pad_maximum_fusion), calls=%async_computation.2 | async-start | bytes 4128768 | tf_op jit(solution)/shard_map/all_to_all | solution.py:83
  101.0 32.6 %all-to-all-done.2 = bf16[16,161,384]{2,1,0:T(8,128)(2,1)} async-done(((bf16[16,161,384]{2,1,0:T(8,128)(2,1)}), bf16[16,161,384]{2,1,0:T(8,128)(2,1)}, u32[]{:S(2)}, u32[]{:S(2)}) %all-to-all-start.2) | async-done | bytes 1978400 | tf_op jit(solution)/shard_map/all_to_all | solution.py:83
  133.6 1.8 %convert_element_type.111 = f32[16,161,384]{2,1,0:T(8,128)S(1)} convert(bf16[16,161,384]{2,1,0:T(8,128)(2,1)} %all-to-all-done.2) | non-fusion elementwise | flops 989184 | bytes 5935104 | tf_op jit(solution)/shard_map/convert_element_type | solution.py:83
  136.0 0.8 pad_maximum_fusion.2
  136.8 4.7 %all-to-all-start.3 = ((bf16[32,6,384]{2,1,0:T(8,128)(2,1)}), bf16[32,6,384]{2,1,0:T(8,128)(2,1)S(1)}, u32[]{:S(2)}, u32[]{:S(2)}) async-start(bf16[32,6,384]{2,1,0:T(8,128)(2,1)} %pad_maximum_fusion.2), calls=%async_computation.3 | async-start | bytes 393216 | tf_op jit(solution)/shard_map/all_to_all | solution.py:97
  141.6 18.8 %all-to-all-done.3 = bf16[32,6,384]{2,1,0:T(8,128)(2,1)S(1)} async-done(((bf16[32,6,384]{2,1,0:T(8,128)(2,1)}), bf16[32,6,384]{2,1,0:T(8,128)(2,1)S(1)}, u32[]{:S(2)}, u32[]{:S(2)}) %all-to-all-start.3) | async-done | bytes 147488 | tf_op jit(solution)/shard_map/all_to_all | solution.py:97
  160.6 0.2 fusion.22
  161.2 0.8 multiply_reduce_fusion.1
  162.0 0.6 copy.63
  162.6 0.7 reduce_sum.110
  (48 shorter events, 2.5 us)
Async XLA Ops:
  0.6 82.6 %copy-start = (bf16[1,6144,128]{2,1,0:T(8,128)(2,1)S(1)}, bf16[1,6144,128]{2,1,0:T(8,128)(2,1)}, u32[]{:S(2)}) copy-start(bf16[1,6144,128]{2,1,0:T(8,128)(2,1)} %param.11) | copy-start | bytes 4718596
  72.3 8.5 %collective-permute-start = (bf16[160,6144]{1,0:T(8,128)(2,1)S(1)}, bf16[160,6144]{1,0:T(8,128)(2,1)}, u32[]{:S(2)}, u32[]{:S(2)}) collective-permute-start(bf16[160,6144]{1,0:T(8,128)(2,1)S(1)} %bitcast.47), channel_id=1, source_target_pairs={{0,4},{4,0},{8,12},{12,8},{16,20},{20,16},{24,28},{28,24},{32,36},... | collective-permute-start | bytes 5898248 | tf_op jit(solution)/shard_map/ppermute | solution.py:45
  77.1 5.5 %copy-start.2 = (bf16[1,6144,128]{2,1,0:T(8,128)(2,1)S(1)}, bf16[1,6144,128]{2,1,0:T(8,128)(2,1)}, u32[]{:S(2)}) copy-start(bf16[1,6144,128]{2,1,0:T(8,128)(2,1)} %param.10) | copy-start | bytes 4718596
  83.3 1.4 copy-start.1
  87.5 5.9 %collective-permute-start.1 = (bf16[160,6144]{1,0:T(8,128)(2,1)S(1)}, bf16[160,6144]{1,0:T(8,128)(2,1)S(1)}, u32[]{:S(2)}, u32[]{:S(2)}) collective-permute-start(bf16[160,6144]{1,0:T(8,128)(2,1)S(1)} %get-tuple-element.36), channel_id=1, source_target_pairs={{0,4},{4,0},{8,12},{12,8},{16,20},{20,16},{24,28},{28,24},{32,36},... | collective-permute-start | bytes 5898248 | tf_op jit(solution)/shard_map/ppermute | solution.py:72
  96.5 37.1 %all-to-all-start.2 = ((bf16[16,161,384]{2,1,0:T(8,128)(2,1)}), bf16[16,161,384]{2,1,0:T(8,128)(2,1)}, u32[]{:S(2)}, u32[]{:S(2)}) async-start(bf16[16,161,384]{2,1,0:T(8,128)(2,1)} %pad_maximum_fusion), calls=%async_computation.2 | async-start | bytes 4128768 | tf_op jit(solution)/shard_map/all_to_all | solution.py:83
  135.4 6.1 %copy-start.3 = (f32[16,2]{0,1:T(2,128)S(1)}, f32[16,2]{0,1:T(2,128)}, u32[]{:S(2)}) copy-start(f32[16,2]{0,1:T(2,128)} %param.9) | copy-start | bytes 388
  136.8 23.6 %all-to-all-start.3 = ((bf16[32,6,384]{2,1,0:T(8,128)(2,1)}), bf16[32,6,384]{2,1,0:T(8,128)(2,1)S(1)}, u32[]{:S(2)}, u32[]{:S(2)}) async-start(bf16[32,6,384]{2,1,0:T(8,128)(2,1)} %pad_maximum_fusion.2), calls=%async_computation.3 | async-start | bytes 393216 | tf_op jit(solution)/shard_map/all_to_all | solution.py:97

commit v10 on v6

--- a/solution.py
+++ b/solution.py
@@ -36,7 +36,10 @@
     pair = jnp.stack(
         [picked.reshape(experts, capacity, feat), scaled.reshape(experts, capacity, feat)], axis=1
     )
-    send = jnp.concatenate([pair] * (group // 2), axis=1).reshape(devices_all, capacity, feat)
+    lanes = 128
+    send = jnp.concatenate([pair] * (group // 2), axis=1).reshape(
+        devices_all, capacity * feat // lanes, lanes
+    )
     recv = lax.all_to_all(send, "expert", split_axis=0, concat_axis=0, tiled=True)
     recv = recv.reshape(rows_n, feat)
     spread = jnp.broadcast_to(recv[None], (planes,) + recv.shape)
@@ -88,17 +91,23 @@
         [
             back_hi.reshape(devices_all, capacity),
             back_lo.reshape(devices_all, capacity),
-            jnp.zeros((devices_all, feat - 2 * capacity), jnp.bfloat16),
+            jnp.zeros((devices_all, lanes - 2 * capacity), jnp.bfloat16),
         ],
         axis=1,
-    ).reshape(devices_all, 1, feat)
-    back_send = jnp.concatenate([shares.reshape(devices_all, capacity, feat), back_dots], axis=1)
+    )
+    back_send = jnp.concatenate(
+        [shares.reshape(devices_all, capacity * feat), back_dots], axis=1
+    ).reshape(devices_all, capacity * feat // lanes + 1, lanes)
     back = lax.all_to_all(back_send, "expert", split_axis=0, concat_axis=0, tiled=True)
-    back = back.astype(jnp.float32).reshape(experts, group // 2, 2, capacity + 1, feat)
-    back_rows = jnp.sum(back[:, :, :, :capacity], axis=1).astype(jnp.bfloat16)
+    back = back.reshape(devices_all, capacity * feat + lanes)
+    back_part = back[:, : capacity * feat].astype(jnp.float32)
+    back_part = back_part.reshape(experts, group // 2, 2, capacity, feat)
+    back_tail = back[:, capacity * feat : capacity * feat + 2 * capacity].astype(jnp.float32)
+    back_tail = back_tail.reshape(experts, group // 2, 2, 2 * capacity)
+    back_rows = jnp.sum(back_part, axis=1).astype(jnp.bfloat16)
     back_rows = back_rows.transpose(0, 2, 1, 3).reshape(slots, 2 * feat)
     slot_dots = jnp.sum(
-        back[:, :, 0, capacity, :capacity] + back[:, :, 0, capacity, capacity:2 * capacity], axis=1
+        back_tail[:, :, 0, :capacity] + back_tail[:, :, 0, capacity:], axis=1
     ).reshape(slots)
     assign = picks.T.astype(jnp.bfloat16)
     a_both = jnp.dot(assign, back_rows, preferred_element_type=jnp.float32)

time: 164 us -> 152 us (0.927)
  waiting for transfers between devices: 54 us -> 23.4 us
  blocking collectives: 67 us -> 93.4 us
  starting transfers between devices: 18.2 us -> 13.1 us
  other arithmetic: 10 us -> 6.3 us
    all_to_all x0 -> x1, blocking collectives: none -> 29.1 us  [per_device(): lax.all_to_all(terms, ('pipe', 'tensor'), 0, 0, tiled=True)]
    all_to_all x1 -> x0, waiting for transfers between devices: 27.7 us -> none  [per_device(): lax.all_to_all(terms, ('pipe', 'tensor'), 0, 0, tiled=True)]
    all_to_all x1 -> x0, starting transfers between devices: 4.42 us -> none  [per_device(): lax.all_to_all(terms, ('pipe', 'tensor'), 0, 0, tiled=True)]
    all_to_all x1, waiting for transfers between devices: 18.8 us -> 15.8 us  [per_device(): lax.all_to_all(back_send, 'expert', split_axis=0, concat_axis=0, tiled=True)]
    all_to_all x1, blocking collectives: 35.2 us -> 32.4 us  [per_device(): lax.all_to_all(send, 'expert', split_axis=0, concat_axis=0, tiled=True)]
  transfers between devices with their start and end apart: 4 -> 3, of which waited for: 4 -> 3; matrix products, arithmetic and copies ran while one was open for 0% -> 0% of each run, Pallas kernels for 0% -> 0%
where the time goes in v10:
time: 152 us; the launch traced here: 151 us
  blocking collectives  93.4 us (61%)
  waiting for transfers between devices  23.4 us (15%)
  starting transfers between devices  13.1 us (9%)
  matrix products  9.27 us (6%)
  other arithmetic  6.3 us (4%)
  local copies, waits for them, and re-layouts  4.95 us (3%)
    all_to_all x1, blocking collectives, per_device(): lax.all_to_all(send, 'expert', split_axis=0, concat_axis=0, tiled=True)  32.4 us
    all_to_all x1, blocking collectives, per_device(): gathered = lax.all_to_all(spread, ('pipe', 'tensor'), 0, 0, tiled=True)  31.9 us
    all_to_all x1, blocking collectives, per_device(): lax.all_to_all(terms, ('pipe', 'tensor'), 0, 0, tiled=True)  29.1 us
    all_to_all x1, waiting for transfers between devices, per_device(): lax.all_to_all(back_send, 'expert', split_axis=0, concat_axis=0, tiled=True)  15.8 us
    all_to_all x1, starting transfers between devices, per_device(): lax.all_to_all(back_send, 'expert', split_axis=0, concat_axis=0, tiled=True)  6.46 us
    ppermute x1, starting transfers between devices, per_device(): other_rows = lax.ppermute(own_rows, 'expert', partner)  4.69 us
    ppermute x1, waiting for transfers between devices, per_device(): got = lax.ppermute(give, 'expert', partner)  3.94 us
    ppermute x1, waiting for transfers between devices, per_device(): other_rows = lax.ppermute(own_rows, 'expert', partner)  3.7 us
  transfers between devices with their start and end apart: 3, of which 3 were waited for; matrix products, arithmetic and copies ran while one was open for 0% of the time, Pallas kernels for 0%

profile of v10, /device:TPU:1, one launch (start us, length us, event | category | flops | bytes accessed | tf_op | source)
XLA Modules:
  0.0 151.4 jit_solution(13873084684739515095)
XLA Ops:
  0.6 0.9 copy.48
  1.7 0.2 select_reduce_fusion.2
  2.1 0.7 multiply_add_fusion
  2.8 0.8 select_reduce_fusion.1
  3.6 0.9 fusion.16
  4.8 32.4 %all_to_all.20 = bf16[32,15,128]{2,1,0:T(8,128)(2,1)S(1)} all-to-all(bf16[32,15,128]{2,1,0:T(8,128)(2,1)S(1)} %reshape.89), channel_id=1, replica_groups=mesh['pipe'=4,'expert'=32,'tensor'=4] {'expert'}, dimensions={0} | all-to-all | bytes 245760 | tf_op jit(solution)/shard_map/all_to_all | solution.py:43
  37.5 31.9 %all_to_all.21 = bf16[16,160,384]{2,1,0:T(8,128)(2,1)S(1)} all-to-all(bf16[16,160,384]{2,1,0:T(8,128)(2,1)S(1)} %broadcast_in_dim.11), channel_id=1, replica_groups=mesh['pipe'=4,'expert'=32,'tensor'=4] {'pipe','tensor'}, dimensions={0} | all-to-all | bytes 3932160 | tf_op jit(solution)/shard_map/all_to_all | solution.py:46
  69.4 0.3 copy.57
  69.7 4.7 %collective-permute-start = (bf16[160,6144]{1,0:T(8,128)(2,1)S(1)}, bf16[160,6144]{1,0:T(8,128)(2,1)}, u32[]{:S(2)}, u32[]{:S(2)}) collective-permute-start(bf16[160,6144]{1,0:T(8,128)(2,1)S(1)} %bitcast.41), channel_id=1, source_target_pairs={{0,4},{4,0},{8,12},{12,8},{16,20},{20,16},{24,28},{28,24},{32,36},... | collective-permute-start | bytes 5898248 | tf_op jit(solution)/shard_map/ppermute | solution.py:48
  74.4 3.7 %collective-permute-done = bf16[160,6144]{1,0:T(8,128)(2,1)} collective-permute-done((bf16[160,6144]{1,0:T(8,128)(2,1)S(1)}, bf16[160,6144]{1,0:T(8,128)(2,1)}, u32[]{:S(2)}, u32[]{:S(2)}) %collective-permute-start) | collective-permute-done | bytes 1966112 | tf_op jit(solution)/shard_map/ppermute | solution.py:48
  78.1 2.8 %fusion.10 = f32[160,128]{1,0:T(8,128)S(1)} fusion(bf16[1,6144,128]{2,1,0:T(8,128)(2,1)} %param.10, bf16[160,6144]{1,0:T(8,128)(2,1)S(1)} %bitcast.42, bf16[160,6144]{1,0:T(8,128)(2,1)} %collective-permute-done, pred[]{:T(512)S(6)} %eq.45), kind=kOutput, calls=%fused_computation.21 | convolution fusion | flops 252641280 | bytes 5586945 | tf_op jit(solution)/shard_map/dot_general | solution.py:55
  81.0 2.5 %fusion.6 = f32[160,128]{1,0:T(8,128)S(1)} fusion(bf16[1,6144,128]{2,1,0:T(8,128)(2,1)S(1)} %copy-done, bf16[160,6144]{1,0:T(8,128)(2,1)S(1)} %bitcast.43, bf16[160,6144]{1,0:T(8,128)(2,1)} %collective-permute-done, pred[]{:T(512)S(6)} %eq.45), kind=kOutput, calls=%fused_computation.17 | convolution fusion | flops 252641280 | bytes 5586945 | tf_op jit(solution)/shard_map/dot_general | solution.py:56
  83.5 0.7 convolution_convert_fusion
  84.2 0.7 fusion.2
  84.9 0.7 copy-done.2
  85.6 0.7 fusion.8
  86.3 0.8 broadcast_select_fusion
  87.1 1.9 %collective-permute-start.1 = (bf16[160,6144]{1,0:T(8,128)(2,1)S(1)}, bf16[160,6144]{1,0:T(8,128)(2,1)S(1)}, u32[]{:S(2)}, u32[]{:S(2)}) collective-permute-start(bf16[160,6144]{1,0:T(8,128)(2,1)S(1)} %get-tuple-element.30), channel_id=1, source_target_pairs={{0,4},{4,0},{8,12},{12,8},{16,20},{20,16},{24,28},{28,24},{32,36},... | collective-permute-start | bytes 5898248 | tf_op jit(solution)/shard_map/ppermute | solution.py:74
  89.0 3.9 %collective-permute-done.1 = bf16[160,6144]{1,0:T(8,128)(2,1)S(1)} collective-permute-done((bf16[160,6144]{1,0:T(8,128)(2,1)S(1)}, bf16[160,6144]{1,0:T(8,128)(2,1)S(1)}, u32[]{:S(2)}, u32[]{:S(2)}) %collective-permute-start.1) | collective-permute-done | bytes 1966112 | tf_op jit(solution)/shard_map/ppermute | solution.py:74
  92.9 1.8 %fusion.1 = (bf16[160,6144]{1,0:T(8,128)(2,1)S(1)}, f32[160]{0:T(256)S(1)}) fusion(bf16[160,6144]{1,0:T(8,128)(2,1)S(1)} %collective-permute-done.1, bf16[160,6144]{1,0:T(8,128)(2,1)S(1)} %convolution_convert_fusion, bf16[160,6144]{1,0:T(8,128)(2,1)S(1)} %get-tuple-element.31, pred[]{:T(512)S(6)} %eq.45, bf16[160,6144]{1,0:T(8,128)(2,1)} %collective-permute-done, ...), kind=kLoop, calls=%fused_computation.6 | loop fusion | flops 8847200 | bytes 11797121 | tf_op jit(solution)/shard_map/convert_element_type | solution.py:76
  94.7 0.2 copy.63
  95.0 0.2 pad_maximum_fusion
  95.3 29.1 %all_to_all.22 = bf16[16,161,384]{2,1,0:T(8,128)(2,1)S(1)} all-to-all(bf16[16,161,384]{2,1,0:T(8,128)(2,1)S(1)} %pad_maximum_fusion), channel_id=1, replica_groups=mesh['pipe'=4,'expert'=32,'tensor'=4] {'pipe','tensor'}, dimensions={0} | all-to-all | bytes 3956736 | tf_op jit(solution)/shard_map/all_to_all | solution.py:85
  124.3 0.3 convert_element_type.112
  125.2 0.7 copy.58
  125.9 6.5 %all-to-all-start.3 = ((bf16[32,16,128]{2,1,0:T(8,128)(2,1)}), bf16[32,16,128]{2,1,0:T(8,128)(2,1)S(1)}, u32[]{:S(2)}, u32[]{:S(2)}) async-start(bf16[32,16,128]{2,1,0:T(8,128)(2,1)} %bitcast.13), calls=%async_computation.3 | async-start | bytes 262144 | tf_op jit(solution)/shard_map/all_to_all | solution.py:101
  132.5 15.8 %all-to-all-done.3 = bf16[32,16,128]{2,1,0:T(8,128)(2,1)S(1)} async-done(((bf16[32,16,128]{2,1,0:T(8,128)(2,1)}), bf16[32,16,128]{2,1,0:T(8,128)(2,1)S(1)}, u32[]{:S(2)}, u32[]{:S(2)}) %all-to-all-start.3) | async-done | bytes 131104 | tf_op jit(solution)/shard_map/all_to_all | solution.py:101
  148.6 0.2 fusion.22
  149.1 0.2 select_reduce_fusion
  149.3 0.8 multiply_reduce_fusion.1
  150.1 0.6 copy.55
  150.7 0.7 reduce_sum.110
  (49 shorter events, 2.4 us)
Async XLA Ops:
  0.6 80.4 %copy-start = (bf16[1,6144,128]{2,1,0:T(8,128)(2,1)S(1)}, bf16[1,6144,128]{2,1,0:T(8,128)(2,1)}, u32[]{:S(2)}) copy-start(bf16[1,6144,128]{2,1,0:T(8,128)(2,1)} %param.11) | copy-start | bytes 4718596
  69.7 8.4 %collective-permute-start = (bf16[160,6144]{1,0:T(8,128)(2,1)S(1)}, bf16[160,6144]{1,0:T(8,128)(2,1)}, u32[]{:S(2)}, u32[]{:S(2)}) collective-permute-start(bf16[160,6144]{1,0:T(8,128)(2,1)S(1)} %bitcast.41), channel_id=1, source_target_pairs={{0,4},{4,0},{8,12},{12,8},{16,20},{20,16},{24,28},{28,24},{32,36},... | collective-permute-start | bytes 5898248 | tf_op jit(solution)/shard_map/ppermute | solution.py:48
  81.0 2.5 %copy-start.1 = (bf16[1,128,6144]{2,1,0:T(8,128)(2,1)S(1)}, bf16[1,128,6144]{2,1,0:T(8,128)(2,1)}, u32[]{:S(2)}) copy-start(bf16[1,128,6144]{2,1,0:T(8,128)(2,1)} %param.12) | copy-start | bytes 4718596
  84.2 1.4 copy-start.2
  87.1 5.9 %collective-permute-start.1 = (bf16[160,6144]{1,0:T(8,128)(2,1)S(1)}, bf16[160,6144]{1,0:T(8,128)(2,1)S(1)}, u32[]{:S(2)}, u32[]{:S(2)}) collective-permute-start(bf16[160,6144]{1,0:T(8,128)(2,1)S(1)} %get-tuple-element.30), channel_id=1, source_target_pairs={{0,4},{4,0},{8,12},{12,8},{16,20},{20,16},{24,28},{28,24},{32,36},... | collective-permute-start | bytes 5898248 | tf_op jit(solution)/shard_map/ppermute | solution.py:74
  124.6 7.8 %copy-start.3 = (f32[16,2]{0,1:T(2,128)S(1)}, f32[16,2]{0,1:T(2,128)}, u32[]{:S(2)}) copy-start(f32[16,2]{0,1:T(2,128)} %param.9) | copy-start | bytes 388
  125.9 22.3 %all-to-all-start.3 = ((bf16[32,16,128]{2,1,0:T(8,128)(2,1)}), bf16[32,16,128]{2,1,0:T(8,128)(2,1)S(1)}, u32[]{:S(2)}, u32[]{:S(2)}) async-start(bf16[32,16,128]{2,1,0:T(8,128)(2,1)} %bitcast.13), calls=%async_computation.3 | async-start | bytes 262144 | tf_op jit(solution)/shard_map/all_to_all | solution.py:101
